TPU v7x, 512 devices: a whole 4x4x16 slice. The times are simulated.
512 devices in a mesh: pipe: 8 (over z_hi, y), expert: 64 (over z_lo, x, core).
Axes of the slice: x: 4, y: 4, z: 16 (z_hi: 2, z_lo: 8; z = z_hi * 8 + z_lo), core: 2. Of those that a mesh axis runs over, the one named last changes fastest.
Arguments:
- tokens: bfloat16 [65536, 2048], P(('pipe', 'expert')), may hold values from -6 to 6
- cotangent: bfloat16 [65536, 2048], P(('pipe', 'expert')), may hold values from -6 to 6
- expert_ids: int32 [65536, 8], P(('pipe', 'expert')), may hold values from 0 to 127, all different within a row
- gates: float32 [65536, 8], P(('pipe', 'expert')), may hold values from 0.05 to 0.5
- w_gate: bfloat16 [8, 2048, 12288], P('pipe', None, 'expert'), as said below
- w_up: bfloat16 [8, 2048, 12288], P('pipe', None, 'expert'), as said below
- w_down: bfloat16 [8, 12288, 2048], P('pipe', 'expert'), as said below
Outputs:
- mixed_out: bfloat16 [65536, 2048], P(('pipe', 'expert'))
- token_grad: bfloat16 [65536, 2048], P(('pipe', 'expert'))
- gate_grad: float32 [65536, 8], P(('pipe', 'expert'))
- down_grad: bfloat16 [8, 12288, 1024], P('pipe', 'expert')
Inputs may be any that keep to these rules, and one draw needn't show every extreme that they name: `expert_ids`: each row names 8 different experts. `w_gate`: the blocks of pipe index p and 7 - p are equal. `w_up`: the blocks of pipe index p and 7 - p are equal. `w_down`: the blocks of pipe index p and 7 - p are equal.
All inputs are finite; a program needn't handle non-finite values.
Results may differ from a plain program's by a relative error of at most 0.0065.
Values may be sent and summed in bfloat16 or wider, within the bound.
No kernel may reach another device: no remote copies, remote signals or barrier semaphores. Data moves between devices by JAX's collectives and lax.ppermute only.
A program may use at most 64 MiB of HBM per device.

v0:
```python
import jax
import jax.numpy as jnp
from jax import lax
from jax.sharding import PartitionSpec as P

WS = 4


def from_partner(block, axis, stride):
    count = lax.axis_size(axis)
    route = []
    for low in range(count):
        high = low | 1 << stride
        if high != low and high < count:
            route += [(low, high), (high, low)]
    return lax.ppermute(block, axis, route)


def silu_parts(preact):
    sigmoid_val = jax.nn.sigmoid(preact)
    return (preact * sigmoid_val, sigmoid_val * (1.0 + preact * (1.0 - sigmoid_val)))


def expert_rows(inputs, scaled, gate_cols, up_cols, down_rows):
    transposed = (((1,), (1,)), ((), ()))
    gate_pre = jnp.dot(inputs, gate_cols, preferred_element_type=jnp.float32)
    up_pre = jnp.dot(inputs, up_cols, preferred_element_type=jnp.float32)
    activated, slope_val = silu_parts(gate_pre)
    hidden = (activated * up_pre).astype(jnp.bfloat16)
    group_out = jnp.dot(hidden, down_rows, preferred_element_type=jnp.float32).astype(jnp.bfloat16)
    hidden_grad = lax.dot_general(scaled, down_rows, transposed, preferred_element_type=jnp.float32)
    grad_gate = (hidden_grad * up_pre * slope_val).astype(jnp.bfloat16)
    grad_up = (hidden_grad * activated).astype(jnp.bfloat16)
    back_gate = lax.dot_general(
        grad_gate, gate_cols, transposed, preferred_element_type=jnp.float32
    )
    back_up = lax.dot_general(grad_up, up_cols, transposed, preferred_element_type=jnp.float32)
    group_grad = (back_gate + back_up).astype(jnp.bfloat16)
    return (hidden, group_out, group_grad)


def split_half(stacked, upper_half):
    half_width = stacked.shape[-1] // 2
    lower_part = stacked[..., :half_width]
    upper_part = stacked[..., half_width:]
    kept_half = jnp.where(upper_half, upper_part, lower_part)
    sent_half = jnp.where(upper_half, lower_part, upper_part)
    return (kept_half, sent_half)


def body(tokens, cotangent, expert_ids, gates, w_gate, w_up, w_down):
    highest = lax.Precision.HIGHEST
    tok_count, model_width = tokens.shape
    chosen_count = expert_ids.shape[1]
    devices = lax.axis_size("expert")
    shards = WS
    experts_here = devices // shards
    capacity = tok_count // 24
    slot_count = experts_here * capacity
    flat_ids = expert_ids.reshape(-1)
    window_ids = jnp.arange(experts_here, dtype=jnp.int32)
    onehot = (flat_ids[:, None] == window_ids[None, :]).astype(jnp.int32)
    earlier = jnp.cumsum(onehot, axis=0) - onehot
    slot_rank = jnp.sum(earlier * onehot, axis=1)
    in_window = (flat_ids < experts_here) & (slot_rank < capacity)
    target_slot = jnp.where(in_window, flat_ids * capacity + slot_rank, slot_count)
    slot_numbers = jnp.arange(slot_count, dtype=jnp.int32)
    pick_pair = (target_slot[None, :] == slot_numbers[:, None]).astype(jnp.float32)
    pick_token = pick_pair.reshape(slot_count, tok_count, chosen_count).sum(axis=2)
    slot_gate = jnp.dot(pick_pair, gates.reshape(-1), precision=highest)
    pick_narrow = pick_token.astype(jnp.bfloat16)
    slot_rows = jnp.dot(pick_narrow, tokens, preferred_element_type=jnp.float32).astype(
        jnp.bfloat16
    )
    slot_cot = jnp.dot(pick_narrow, cotangent, preferred_element_type=jnp.float32)
    slot_scaled = (slot_gate[:, None] * slot_cot).astype(jnp.bfloat16)

    def spread(rows):
        shaped = rows.reshape(experts_here, 1, capacity, model_width)
        return jnp.broadcast_to(shaped, (experts_here, shards, capacity, model_width)).reshape(
            devices, capacity, model_width
        )

    gate_cols = w_gate[0]
    up_cols = w_up[0]
    down_rows = w_down[0]
    inputs = lax.all_to_all(spread(slot_rows), "expert", split_axis=0, concat_axis=0, tiled=True)
    scaled = lax.all_to_all(spread(slot_scaled), "expert", split_axis=0, concat_axis=0, tiled=True)
    sources, item_count, _ = inputs.shape
    hidden, group_out, group_grad = expert_rows(
        inputs.reshape(-1, model_width),
        scaled.reshape(-1, model_width),
        gate_cols,
        up_cols,
        down_rows,
    )
    hidden = hidden.reshape(sources, item_count, -1)
    stacked = jnp.stack(
        [
            group_out.reshape(sources, item_count, model_width),
            group_grad.reshape(sources, item_count, model_width),
        ]
    )
    back_out = lax.all_to_all(stacked[0], "expert", split_axis=0, concat_axis=0, tiled=True)
    back_grad = lax.all_to_all(stacked[1], "expert", split_axis=0, concat_axis=0, tiled=True)
    back_out, back_grad, hidden, scaled = (back_out, back_grad, hidden, scaled)
    expert_out = (
        back_out.reshape(experts_here, shards, capacity, model_width)
        .astype(jnp.float32)
        .sum(axis=1)
        .reshape(slot_count, model_width)
    )
    grad_terms = (
        back_grad.reshape(experts_here, shards, capacity, model_width)
        .astype(jnp.float32)
        .sum(axis=1)
        .reshape(slot_count, model_width)
    )
    weighted = slot_gate[:, None] * expert_out
    mixed_out = jnp.dot(pick_token.T, weighted, precision=highest).astype(jnp.bfloat16)
    slot_value = jnp.sum(slot_cot * expert_out, axis=1)
    gate_grad = jnp.dot(slot_value, pick_pair, precision=highest).reshape(tok_count, chosen_count)
    token_grad = jnp.dot(pick_token.T, grad_terms, precision=highest).astype(jnp.bfloat16)
    local_down = lax.dot_general(
        hidden.reshape(-1, hidden.shape[-1]),
        scaled.reshape(-1, model_width),
        (((0,), (0,)), ((), ())),
        preferred_element_type=jnp.float32,
    ).astype(jnp.bfloat16)
    sections = lax.axis_size("pipe")
    section_pos = lax.axis_index("pipe")
    kept_half, sent_half = split_half(local_down, section_pos >= sections // 2)
    travelled = sent_half
    for bit_pos in range(sections.bit_length() - 1):
        travelled = from_partner(travelled, "pipe", bit_pos)
    partner_part = travelled.astype(jnp.float32)
    down_grad = (kept_half.astype(jnp.float32) + partner_part).astype(jnp.bfloat16)[None]
    return (mixed_out, token_grad, gate_grad, down_grad)


def solution(mesh):
    placed = (
        P(("pipe", "expert"), None),
        P(("pipe", "expert"), None),
        P(("pipe", "expert"), None),
        P(("pipe", "expert"), None),
        P("pipe", None, "expert"),
        P("pipe", None, "expert"),
        P("pipe", "expert", None),
    )
    return jax.shard_map(
        body,
        mesh=mesh,
        in_specs=placed,
        out_specs=(
            P(("pipe", "expert"), None),
            P(("pipe", "expert"), None),
            P(("pipe", "expert"), None),
            P("pipe", "expert", None),
        ),
        check_vma=False,
    )
```

profile of v0, /device:TPU:1, one launch (start us, length us, event | category | flops | bytes accessed | tf_op | source)
XLA Modules:
  0.0 495.0 jit_solution(5450255913457392212)
XLA Ops:
  1.7 4.5 reduce-window.6
  9.9 112.4 %all_to_all.20 = bf16[64,5,2048]{2,1,0:T(8,128)(2,1)} all-to-all(bf16[64,5,2048]{2,1,0:T(8,128)(2,1)S(1)} %bitcast.63), channel_id=1, replica_groups=mesh['pipe'=8,'expert'=64] {'expert'}, dimensions={0} | all-to-all | bytes 2621440 | tf_op jit(solution)/shard_map/all_to_all | solution.py:87
  122.3 2.6 reshape.95
  128.3 1.6 squeeze_stack_reshape.6
  129.9 8.9 %all-to-all-start.1 = ((bf16[64,5,2048]{2,1,0:T(8,128)(2,1)}), bf16[64,5,2048]{2,1,0:T(8,128)(2,1)S(1)}, u32[]{:S(2)}, u32[]{:S(2)}) async-start(bf16[64,5,2048]{2,1,0:T(8,128)(2,1)} %squeeze_stack_reshape.6), calls=%async_computation.1 | async-start | bytes 4194304 | tf_op jit(solution)/shard_map/all_to_all | solution.py:104
  139.2 95.0 %all-to-all-done.1 = bf16[64,5,2048]{2,1,0:T(8,128)(2,1)S(1)} async-done(((bf16[64,5,2048]{2,1,0:T(8,128)(2,1)}), bf16[64,5,2048]{2,1,0:T(8,128)(2,1)S(1)}, u32[]{:S(2)}, u32[]{:S(2)}) %all-to-all-start.1) | async-done | bytes 1310752 | tf_op jit(solution)/shard_map/all_to_all | solution.py:104
  234.3 1.5 convert_reduce_fusion.1
  237.9 104.1 %all_to_all.21 = bf16[64,5,2048]{2,1,0:T(8,128)(2,1)} all-to-all(bf16[64,5,2048]{2,1,0:T(8,128)(2,1)S(1)} %bitcast.64), channel_id=1, replica_groups=mesh['pipe'=8,'expert'=64] {'expert'}, dimensions={0} | all-to-all | bytes 2621440 | tf_op jit(solution)/shard_map/all_to_all | solution.py:88
  342.0 2.6 reshape.98
  344.6 1.9 fusion.1
  347.1 1.6 fusion
  348.8 3.4 squeeze_stack_reshape.7
  352.2 8.9 %all-to-all-start.3 = ((bf16[64,5,2048]{2,1,0:T(8,128)(2,1)}), bf16[64,5,2048]{2,1,0:T(8,128)(2,1)}, u32[]{:S(2)}, u32[]{:S(2)}) async-start(bf16[64,5,2048]{2,1,0:T(8,128)(2,1)} %squeeze_stack_reshape.7), calls=%async_computation.3 | async-start | bytes 4194304 | tf_op jit(solution)/shard_map/all_to_all | solution.py:105
  361.1 1.5 convolution_convert_fusion.1
  362.6 3.2 collective-permute-start
  365.8 8.9 %collective-permute-done = bf16[192,1024]{1,0:T(8,128)(2,1)S(1)} collective-permute-done((bf16[192,1024]{1,0:T(8,128)(2,1)S(1)}, bf16[192,1024]{1,0:T(8,128)(2,1)S(1)}, u32[]{:S(2)}, u32[]{:S(2)}) %collective-permute-start) | collective-permute-done | bytes 393248 | tf_op jit(solution)/shard_map/ppermute | solution.py:16
  374.8 4.8 collective-permute-start.1
  379.7 8.0 %collective-permute-done.1 = bf16[192,1024]{1,0:T(8,128)(2,1)S(1)} collective-permute-done((bf16[192,1024]{1,0:T(8,128)(2,1)S(1)}, bf16[192,1024]{1,0:T(8,128)(2,1)S(1)}, u32[]{:S(2)}, u32[]{:S(2)}) %collective-permute-start.1) | collective-permute-done | bytes 393248 | tf_op jit(solution)/shard_map/ppermute | solution.py:16
  387.7 8.1 %collective-permute-start.2 = (bf16[192,1024]{1,0:T(8,128)(2,1)S(1)}, bf16[192,1024]{1,0:T(8,128)(2,1)S(1)}, u32[]{:S(2)}, u32[]{:S(2)}) collective-permute-start(bf16[192,1024]{1,0:T(8,128)(2,1)S(1)} %collective-permute-done.1), channel_id=1, source_target_pairs={{0,256},{256,0},{64,320},{320,64},{128,384},{384,128},{192,448},{4... | collective-permute-start | bytes 1179656 | tf_op jit(solution)/shard_map/ppermute | solution.py:16
  396.8 2.6 convolution_convert_fusion.3
  399.4 21.6 %collective-permute-done.2 = bf16[192,1024]{1,0:T(8,128)(2,1)S(1)} collective-permute-done((bf16[192,1024]{1,0:T(8,128)(2,1)S(1)}, bf16[192,1024]{1,0:T(8,128)(2,1)S(1)}, u32[]{:S(2)}, u32[]{:S(2)}) %collective-permute-start.2) | collective-permute-done | bytes 393248 | tf_op jit(solution)/shard_map/ppermute | solution.py:16
  422.0 68.2 %all-to-all-done.3 = bf16[64,5,2048]{2,1,0:T(8,128)(2,1)} async-done(((bf16[64,5,2048]{2,1,0:T(8,128)(2,1)}), bf16[64,5,2048]{2,1,0:T(8,128)(2,1)}, u32[]{:S(2)}, u32[]{:S(2)}) %all-to-all-start.3) | async-done | bytes 1310752 | tf_op jit(solution)/shard_map/all_to_all | solution.py:105
  490.2 2.2 convert_reduce_fusion
  493.2 1.8 convolution_convert_fusion.2
  (62 shorter events, 14.0 us)
Async XLA Ops:
  0.6 125.0 %copy-start = (bf16[1,2048,192]{1,2,0:T(8,128)(2,1)S(1)}, bf16[1,2048,192]{1,2,0:T(8,128)(2,1)}, u32[]{:S(2)}) copy-start(bf16[1,2048,192]{1,2,0:T(8,128)(2,1)} %param.12) | copy-start | bytes 2359300
  7.6 0.6 copy-start.6
  122.3 2.6 copy-start.3
  125.7 1.4 copy-start.1
  125.7 2.1 copy-start.5
  127.1 0.7 copy-start.9
  129.9 8.9 %copy-start.12 = (f32[128,8]{0,1:T(8,128)S(1)}, f32[128,8]{0,1:T(8,128)}, u32[]{:S(2)}) copy-start(f32[128,8]{0,1:T(8,128)} %param.10) | copy-start | bytes 12292
  129.9 104.3 %all-to-all-start.1 = ((bf16[64,5,2048]{2,1,0:T(8,128)(2,1)}), bf16[64,5,2048]{2,1,0:T(8,128)(2,1)S(1)}, u32[]{:S(2)}, u32[]{:S(2)}) async-start(bf16[64,5,2048]{2,1,0:T(8,128)(2,1)} %squeeze_stack_reshape.6), calls=%async_computation.1 | async-start | bytes 4194304 | tf_op jit(solution)/shard_map/all_to_all | solution.py:104
  235.7 1.4 copy-start.7
  235.7 1.4 copy-start.10
  344.6 2.0 copy-start.2
  344.6 1.9 copy-start.4
  344.6 1.9 copy-start.11
  352.2 138.0 %all-to-all-start.3 = ((bf16[64,5,2048]{2,1,0:T(8,128)(2,1)}), bf16[64,5,2048]{2,1,0:T(8,128)(2,1)}, u32[]{:S(2)}, u32[]{:S(2)}) async-start(bf16[64,5,2048]{2,1,0:T(8,128)(2,1)} %squeeze_stack_reshape.7), calls=%async_computation.3 | async-start | bytes 4194304 | tf_op jit(solution)/shard_map/all_to_all | solution.py:105
  362.6 12.1 %collective-permute-start = (bf16[192,1024]{1,0:T(8,128)(2,1)S(1)}, bf16[192,1024]{1,0:T(8,128)(2,1)S(1)}, u32[]{:S(2)}, u32[]{:S(2)}) collective-permute-start(bf16[192,1024]{1,0:T(8,128)(2,1)S(1)} %broadcast_select_fusion), channel_id=1, source_target_pairs={{0,64},{64,0},{128,192},{192,128},{256,320},{320,256},{384,448},{4... | collective-permute-start | bytes 1179656 | tf_op jit(solution)/shard_map/ppermute | solution.py:16
  374.8 12.9 %collective-permute-start.1 = (bf16[192,1024]{1,0:T(8,128)(2,1)S(1)}, bf16[192,1024]{1,0:T(8,128)(2,1)S(1)}, u32[]{:S(2)}, u32[]{:S(2)}) collective-permute-start(bf16[192,1024]{1,0:T(8,128)(2,1)S(1)} %collective-permute-done), channel_id=1, source_target_pairs={{0,128},{128,0},{64,192},{192,64},{256,384},{384,256},{320,448},{4... | collective-permute-start | bytes 1179656 | tf_op jit(solution)/shard_map/ppermute | solution.py:16
  387.7 33.4 %collective-permute-start.2 = (bf16[192,1024]{1,0:T(8,128)(2,1)S(1)}, bf16[192,1024]{1,0:T(8,128)(2,1)S(1)}, u32[]{:S(2)}, u32[]{:S(2)}) collective-permute-start(bf16[192,1024]{1,0:T(8,128)(2,1)S(1)} %collective-permute-done.1), channel_id=1, source_target_pairs={{0,256},{256,0},{64,320},{320,64},{128,384},{384,128},{192,448},{4... | collective-permute-start | bytes 1179656 | tf_op jit(solution)/shard_map/ppermute | solution.py:16
  492.4 0.8 copy-start.8
where the time goes:
time: 496 us; the launch traced here: 495 us
  blocking collectives  217 us (44%)
  waiting for transfers between devices  202 us (41%)
  starting transfers between devices  33.9 us (7%)
  local copies, waits for them, and re-layouts  16.9 us (3%)
  matrix products  14.4 us (3%)
  other arithmetic  10.5 us (2%)
    all_to_all x1, blocking collectives, body(): lax.all_to_all(spread(slot_rows), 'expert', split_axis=0, concat_axis=0,...  112 us
    all_to_all x1, blocking collectives, body(): lax.all_to_all(spread(slot_scaled), 'expert', split_axis=0, concat_axis=0...  104 us
    all_to_all x1, waiting for transfers between devices, body(): lax.all_to_all(stacked[0], 'expert', split_axis=0, concat_axis=0, tiled=T...  95 us
    all_to_all x1, waiting for transfers between devices, body(): lax.all_to_all(stacked[1], 'expert', split_axis=0, concat_axis=0, tiled=T...  68.2 us
    ppermute x3, waiting for transfers between devices, from_partner(): return lax.ppermute(block, axis, route)  38.5 us
    ppermute x3, starting transfers between devices, from_partner(): return lax.ppermute(block, axis, route)  16.1 us
  transfers between devices with their start and end apart: 5, of which 5 were waited for; matrix products, arithmetic and copies ran while one was open for 1% of the time, Pallas kernels for 0%

commit v1 on v0

v1 whole, which is shorter than its diff:
```python
import jax
import jax.numpy as jnp
from jax import lax
from jax.sharding import Mesh, PartitionSpec as P

WS = 4


def from_partner(block, axis, stride):
    count = lax.axis_size(axis)
    route = []
    for low in range(count):
        high = low | 1 << stride
        if high != low and high < count:
            route += [(low, high), (high, low)]
    return lax.ppermute(block, axis, route)


def silu_parts(preact):
    sigmoid_val = jax.nn.sigmoid(preact)
    return (preact * sigmoid_val, sigmoid_val * (1.0 + preact * (1.0 - sigmoid_val)))


def expert_rows(inputs, scaled, gate_cols, up_cols, down_rows):
    transposed = (((1,), (1,)), ((), ()))
    gate_pre = jnp.dot(inputs, gate_cols, preferred_element_type=jnp.float32)
    up_pre = jnp.dot(inputs, up_cols, preferred_element_type=jnp.float32)
    activated, slope_val = silu_parts(gate_pre)
    hidden = (activated * up_pre).astype(jnp.bfloat16)
    group_out = jnp.dot(hidden, down_rows, preferred_element_type=jnp.float32).astype(jnp.bfloat16)
    hidden_grad = lax.dot_general(scaled, down_rows, transposed, preferred_element_type=jnp.float32)
    grad_gate = (hidden_grad * up_pre * slope_val).astype(jnp.bfloat16)
    grad_up = (hidden_grad * activated).astype(jnp.bfloat16)
    back_gate = lax.dot_general(
        grad_gate, gate_cols, transposed, preferred_element_type=jnp.float32
    )
    back_up = lax.dot_general(grad_up, up_cols, transposed, preferred_element_type=jnp.float32)
    group_grad = (back_gate + back_up).astype(jnp.bfloat16)
    return (hidden, group_out, group_grad)


def split_half(stacked, upper_half):
    half_width = stacked.shape[-1] // 2
    lower_part = stacked[..., :half_width]
    upper_part = stacked[..., half_width:]
    kept_half = jnp.where(upper_half, upper_part, lower_part)
    sent_half = jnp.where(upper_half, lower_part, upper_part)
    return (kept_half, sent_half)


def body(tokens, cotangent, expert_ids, gates, w_gate, w_up, w_down):
    highest = lax.Precision.HIGHEST
    tok_count, model_width = tokens.shape
    chosen_count = expert_ids.shape[1]
    experts_here = lax.axis_size("eg")
    shards = lax.axis_size("es")
    capacity = tok_count // 24
    slot_count = experts_here * capacity
    flat_ids = expert_ids.reshape(-1)
    window_ids = jnp.arange(experts_here, dtype=jnp.int32)
    onehot = (flat_ids[:, None] == window_ids[None, :]).astype(jnp.int32)
    earlier = jnp.cumsum(onehot, axis=0) - onehot
    slot_rank = jnp.sum(earlier * onehot, axis=1)
    in_window = (flat_ids < experts_here) & (slot_rank < capacity)
    target_slot = jnp.where(in_window, flat_ids * capacity + slot_rank, slot_count)
    slot_numbers = jnp.arange(slot_count, dtype=jnp.int32)
    pick_pair = (target_slot[None, :] == slot_numbers[:, None]).astype(jnp.float32)
    pick_token = pick_pair.reshape(slot_count, tok_count, chosen_count).sum(axis=2)
    slot_gate = jnp.dot(pick_pair, gates.reshape(-1), precision=highest)
    pick_narrow = pick_token.astype(jnp.bfloat16)
    slot_rows = jnp.dot(pick_narrow, tokens, preferred_element_type=jnp.float32).astype(
        jnp.bfloat16
    )
    slot_cot = jnp.dot(pick_narrow, cotangent, preferred_element_type=jnp.float32)
    slot_scaled = (slot_gate[:, None] * slot_cot).astype(jnp.bfloat16)

    payload = jnp.concatenate([slot_rows, slot_scaled], axis=1).reshape(experts_here, -1)
    arrived = lax.all_to_all(payload, "eg", 0, 0, tiled=True)
    copies = jnp.broadcast_to(arrived[None], (shards,) + arrived.shape).reshape(
        shards * experts_here, -1
    )
    gathered = lax.all_to_all(copies, "es", 0, 0, tiled=True)
    gathered = gathered.reshape(shards * experts_here * capacity, 2 * model_width)
    inputs = gathered[:, :model_width]
    scaled = gathered[:, model_width:]
    hidden, group_out, group_grad = expert_rows(
        inputs, scaled, w_gate[0], w_up[0], w_down[0]
    )

    parts = jnp.concatenate([group_out, group_grad], axis=1).reshape(shards, -1)
    parts = lax.all_to_all(parts, "es", 0, 0, tiled=True)
    summed = parts.reshape(shards, -1).astype(jnp.float32).sum(axis=0)
    summed = summed.astype(jnp.bfloat16).reshape(experts_here, -1)
    returned = lax.all_to_all(summed, "eg", 0, 0, tiled=True)
    returned = returned.reshape(slot_count, 2 * model_width).astype(jnp.float32)
    expert_out = returned[:, :model_width]
    grad_terms = returned[:, model_width:]

    weighted = slot_gate[:, None] * expert_out
    mixed_out = jnp.dot(pick_token.T, weighted, precision=highest).astype(jnp.bfloat16)
    slot_value = jnp.sum(slot_cot * expert_out, axis=1)
    gate_grad = jnp.dot(slot_value, pick_pair, precision=highest).reshape(tok_count, chosen_count)
    token_grad = jnp.dot(pick_token.T, grad_terms, precision=highest).astype(jnp.bfloat16)
    local_down = lax.dot_general(
        hidden,
        scaled,
        (((0,), (0,)), ((), ())),
        preferred_element_type=jnp.float32,
    ).astype(jnp.bfloat16)
    sections = lax.axis_size("pipe")
    section_pos = lax.axis_index("pipe")
    kept_half, sent_half = split_half(local_down, section_pos >= sections // 2)
    mirror = [(p, sections - 1 - p) for p in range(sections)]
    partner_part = lax.ppermute(sent_half, "pipe", mirror).astype(jnp.float32)
    down_grad = (kept_half.astype(jnp.float32) + partner_part).astype(jnp.bfloat16)[None]
    return (mixed_out, token_grad, gate_grad, down_grad)


def solution(mesh):
    experts = mesh.shape["expert"]
    split = Mesh(
        mesh.devices.reshape(mesh.shape["pipe"], experts // WS, WS), ("pipe", "eg", "es")
    )
    rows = P(("pipe", "eg", "es"), None)
    placed = (
        rows,
        rows,
        rows,
        rows,
        P("pipe", None, ("eg", "es")),
        P("pipe", None, ("eg", "es")),
        P("pipe", ("eg", "es"), None),
    )
    return jax.shard_map(
        body,
        mesh=split,
        in_specs=placed,
        out_specs=(rows, rows, rows, P("pipe", ("eg", "es"), None)),
        check_vma=False,
    )
```

time: 496 us -> 287 us (0.58)
  the two profiles are of different devices: /device:TPU:1 before, /device:TPU:128 now
where the time goes in v1:
time: 287 us; the launch traced here: 286 us
  blocking collectives  113 us (39%)
  waiting for transfers between devices  55.8 us (19%)
  other arithmetic  52.6 us (18%)
  local copies, waits for them, and re-layouts  27.2 us (9%)
  starting transfers between devices  21.1 us (7%)
  matrix products  15.4 us (5%)
    ppermute x1, waiting for transfers between devices, body(): partner_part = lax.ppermute(sent_half, 'pipe', mirror).astype(jnp.float32)  55.8 us
    all_to_all x1, blocking collectives, body(): arrived = lax.all_to_all(payload, 'eg', 0, 0, tiled=True)  44.6 us
    all_to_all x1, blocking collectives, body(): parts = lax.all_to_all(parts, 'es', 0, 0, tiled=True)  34.9 us
    all_to_all x1, blocking collectives, body(): gathered = lax.all_to_all(copies, 'es', 0, 0, tiled=True)  33.8 us
    all_to_all x1, other arithmetic, body(): parts = lax.all_to_all(parts, 'es', 0, 0, tiled=True)  17.5 us
    reduce_sum x1, other arithmetic, body(): summed = parts.reshape(shards, -1).astype(jnp.float32).sum(axis=0)  14.7 us
    unnamed x23, local copies, waits for them, and re-layouts  14.4 us
    ppermute x1, starting transfers between devices, body(): partner_part = lax.ppermute(sent_half, 'pipe', mirror).astype(jnp.float32)  10.9 us
  transfers between devices with their start and end apart: 2, of which 1 were waited for; matrix products, arithmetic and copies ran while one was open for 1% of the time, Pallas kernels for 0%

profile of v1, /device:TPU:128, one launch (start us, length us, event | category | flops | bytes accessed | tf_op | source)
XLA Modules:
  0.0 286.3 jit_solution(2402453378547567369)
XLA Ops:
  1.7 4.5 %reduce-window.6 = s32[16,8,128]{2,1,0:T(8,128)S(1)} reduce-window(s32[16,8,128]{2,1,0:T(8,128)S(1)} %fusion.27, s32[]{:T(128)} %constant.7.clone.1), window={size=1x1x128 pad=0_0x0_0x127_0}, to_apply=%region_0.0 | reduce-window | flops 2080768 | bytes 131076 | tf_op jit(solution)/shard_map/reduce-window
  8.7 1.3 convolution_convert_fusion.4
  10.1 2.2 multiply_convert_fusion
  13.9 4.6 %reduce.5 = bf16[16,20480]{1,0:T(8,128)(2,1)S(1)} reduce(bf16[16,1,20480]{2,1,0:T(2,128)(2,1)S(1)} %all_to_all.29, bf16[]{:T(256)} %broadcast.78), dimensions={1}, to_apply=%all_to_all.29.reduce_sub_computation | reduce | bytes 1310722 | tf_op jit(solution)/shard_map/all_to_all | solution.py:78
  18.9 44.6 %all_to_all.36 = bf16[16,2,10240]{2,1,0:T(2,128)(2,1)S(1)} all-to-all(bf16[16,2,10240]{2,1,0:T(2,128)(2,1)S(1)} %reshape.99), channel_id=1, replica_groups=mesh['pipe'=8,'eg'=16,'es'=4] {'eg'}, dimensions={0} | all-to-all | bytes 1310720 | tf_op jit(solution)/shard_map/all_to_all | solution.py:78
  65.1 33.8 %all_to_all.37 = bf16[4,16,20480]{2,1,0:T(8,128)(2,1)S(1)} all-to-all(bf16[4,16,20480]{2,1,0:T(8,128)(2,1)S(1)} %broadcast_in_dim.25), channel_id=1, replica_groups=mesh['pipe'=8,'eg'=16,'es'=4] {'es'}, dimensions={0} | all-to-all | bytes 5242880 | tf_op jit(solution)/shard_map/all_to_all | solution.py:82
  98.9 3.6 %reshape.91 = bf16[320,4096]{1,0:T(8,128)(2,1)} reshape(bf16[4,16,20480]{2,1,0:T(8,128)(2,1)S(1)} %all_to_all.37) | data formatting | bytes 5242880 | tf_op jit(solution)/shard_map/reshape | solution.py:83
  102.5 2.3 fusion.6
  104.8 1.8 fusion.2
  110.2 5.1 %all_to_all.30 = bf16[4,1,327680]{2,1,0:T(2,128)(2,1)} reshape(bf16[320,4096]{1,0:T(8,128)(2,1)S(1)} %pad_maximum_fusion) | data formatting | bytes 5242880 | tf_op jit(solution)/shard_map/all_to_all | solution.py:91
  115.4 17.5 %reduce.6 = bf16[4,327680]{1,0:T(4,128)(2,1)S(1)} reduce(bf16[4,1,327680]{2,1,0:T(2,128)(2,1)} %all_to_all.30, bf16[]{:T(256)} %broadcast.78), dimensions={1}, to_apply=%all_to_all.30.reduce_sub_computation | reduce | bytes 5242882 | tf_op jit(solution)/shard_map/all_to_all | solution.py:91
  132.9 4.1 %reshape.101 = bf16[4,2,163840]{2,1,0:T(2,128)(2,1)} reshape(bf16[4,327680]{1,0:T(4,128)(2,1)S(1)} %reduce.6) | data formatting | bytes 5242880
  137.0 34.9 %all_to_all.38 = bf16[4,2,163840]{2,1,0:T(2,128)(2,1)S(1)} all-to-all(bf16[4,2,163840]{2,1,0:T(2,128)(2,1)} %reshape.101), channel_id=1, replica_groups=mesh['pipe'=8,'eg'=16,'es'=4] {'es'}, dimensions={0} | all-to-all | bytes 5242880 | tf_op jit(solution)/shard_map/all_to_all | solution.py:91
  171.9 3.8 %reshape.102 = bf16[4,1,327680]{2,1,0:T(2,128)(2,1)} reshape(bf16[4,2,163840]{2,1,0:T(2,128)(2,1)S(1)} %all_to_all.38) | data formatting | bytes 5242880
  175.7 14.7 %reduce_sum.44 = bf16[327680]{0:T(1024)(128)(2,1)S(1)} reduce(bf16[4,1,327680]{2,1,0:T(2,128)(2,1)} %reshape.102, bf16[]{:T(256)} %constant.22.clone.1), dimensions={0,1}, to_apply=%region_4.5 | reduce | flops 983040 | bytes 3276802 | tf_op jit(solution)/shard_map/reduce_sum | solution.py:92
  190.7 4.6 %reduce.7 = bf16[16,20480]{1,0:T(8,128)(2,1)S(1)} reduce(bf16[16,1,20480]{2,1,0:T(2,128)(2,1)S(1)} %all_to_all.31, bf16[]{:T(256)} %broadcast.78), dimensions={1}, to_apply=%all_to_all.31.reduce_sub_computation | reduce | bytes 1310722 | tf_op jit(solution)/shard_map/all_to_all | solution.py:94
  195.4 1.3 reshape.103
  196.7 10.2 %all-to-all-start.3 = ((bf16[16,2,10240]{2,1,0:T(2,128)(2,1)}), bf16[16,2,10240]{2,1,0:T(2,128)(2,1)S(1)}, u32[]{:S(2)}, u32[]{:S(2)}) async-start(bf16[16,2,10240]{2,1,0:T(2,128)(2,1)} %reshape.103), calls=%async_computation.3 | async-start | bytes 1310720 | tf_op jit(solution)/shard_map/all_to_all | solution.py:94
  206.9 1.9 convolution_convert_fusion.1
  208.8 10.9 %collective-permute-start = (bf16[192,1024]{1,0:T(8,128)(2,1)S(1)}, bf16[192,1024]{1,0:T(8,128)(2,1)S(1)}, u32[]{:S(2)}, u32[]{:S(2)}) collective-permute-start(bf16[192,1024]{1,0:T(8,128)(2,1)S(1)} %broadcast_select_fusion), channel_id=1, source_target_pairs={{0,448},{64,384},{128,320},{192,256},{256,192},{320,128},{384,64},... | collective-permute-start | bytes 1179656 | tf_op jit(solution)/shard_map/ppermute | solution.py:114
  219.9 55.8 %collective-permute-done = bf16[192,1024]{1,0:T(8,128)(2,1)S(1)} collective-permute-done((bf16[192,1024]{1,0:T(8,128)(2,1)S(1)}, bf16[192,1024]{1,0:T(8,128)(2,1)S(1)}, u32[]{:S(2)}, u32[]{:S(2)}) %collective-permute-start) | collective-permute-done | bytes 393248 | tf_op jit(solution)/shard_map/ppermute | solution.py:114
  277.2 4.0 %reduce.3 = bf16[16,20480]{1,0:T(8,128)(2,1)S(1)} reduce(bf16[16,1,20480]{2,1,0:T(2,128)(2,1)S(1)} %reshape.104, bf16[]{:T(256)} %constant.35), dimensions={1}, to_apply=%all_to_all.28.reduce_sub_computation | reduce | bytes 1310722 | tf_op jit(solution)/shard_map/all_to_all | solution.py:94
  281.8 1.4 convolution_convert_fusion.2
  283.3 1.9 convolution_convert_fusion.3
  (55 shorter events, 14.5 us)
Async XLA Ops:
  0.6 106.0 %copy-start = (bf16[1,2048,192]{1,2,0:T(8,128)(2,1)S(1)}, bf16[1,2048,192]{1,2,0:T(8,128)(2,1)}, u32[]{:S(2)}) copy-start(bf16[1,2048,192]{1,2,0:T(8,128)(2,1)} %param.12) | copy-start | bytes 2359300
  102.5 2.4 copy-start.1
  106.7 1.1 copy-start.3
  107.4 1.6 copy-start.5
  108.4 1.1 copy-start.4
  190.7 16.2 %copy-start.6 = (bf16[320,192]{0,1:T(8,128)(2,1)S(1)}, bf16[320,192]{0,1:T(8,128)(2,1)}, u32[]{:S(2)}) copy-start(bf16[320,192]{0,1:T(8,128)(2,1)} %copy-done.5) | copy-start | bytes 368644
  196.7 79.9 %all-to-all-start.3 = ((bf16[16,2,10240]{2,1,0:T(2,128)(2,1)}), bf16[16,2,10240]{2,1,0:T(2,128)(2,1)S(1)}, u32[]{:S(2)}, u32[]{:S(2)}) async-start(bf16[16,2,10240]{2,1,0:T(2,128)(2,1)} %reshape.103), calls=%async_computation.3 | async-start | bytes 1310720 | tf_op jit(solution)/shard_map/all_to_all | solution.py:94
  208.8 66.8 %collective-permute-start = (bf16[192,1024]{1,0:T(8,128)(2,1)S(1)}, bf16[192,1024]{1,0:T(8,128)(2,1)S(1)}, u32[]{:S(2)}, u32[]{:S(2)}) collective-permute-start(bf16[192,1024]{1,0:T(8,128)(2,1)S(1)} %broadcast_select_fusion), channel_id=1, source_target_pairs={{0,448},{64,384},{128,320},{192,256},{256,192},{320,128},{384,64},... | collective-permute-start | bytes 1179656 | tf_op jit(solution)/shard_map/ppermute | solution.py:114
  277.2 7.9 %copy-start.2 = (f32[80,2048]{1,0:T(8,128)S(1)}, f32[80,2048]{1,0:T(8,128)}, u32[]{:S(2)}) copy-start(f32[80,2048]{1,0:T(8,128)} %get-tuple-element.5) | copy-start | bytes 1966084

commit v2 on v1

--- a/solution.py
+++ b/solution.py
@@ -74,10 +74,13 @@
     slot_cot = jnp.dot(pick_narrow, cotangent, preferred_element_type=jnp.float32)
     slot_scaled = (slot_gate[:, None] * slot_cot).astype(jnp.bfloat16)
 
-    payload = jnp.concatenate([slot_rows, slot_scaled], axis=1).reshape(experts_here, -1)
+    tile_rows = 16
+    payload = jnp.concatenate([slot_rows, slot_scaled], axis=1).reshape(
+        experts_here, tile_rows, -1
+    )
     arrived = lax.all_to_all(payload, "eg", 0, 0, tiled=True)
     copies = jnp.broadcast_to(arrived[None], (shards,) + arrived.shape).reshape(
-        shards * experts_here, -1
+        (shards * experts_here,) + arrived.shape[1:]
     )
     gathered = lax.all_to_all(copies, "es", 0, 0, tiled=True)
     gathered = gathered.reshape(shards * experts_here * capacity, 2 * model_width)
@@ -87,10 +90,10 @@
         inputs, scaled, w_gate[0], w_up[0], w_down[0]
     )
 
-    parts = jnp.concatenate([group_out, group_grad], axis=1).reshape(shards, -1)
+    parts = jnp.concatenate([group_out, group_grad], axis=1).reshape(shards, slot_count, -1)
     parts = lax.all_to_all(parts, "es", 0, 0, tiled=True)
-    summed = parts.reshape(shards, -1).astype(jnp.float32).sum(axis=0)
-    summed = summed.astype(jnp.bfloat16).reshape(experts_here, -1)
+    summed = parts.astype(jnp.float32).sum(axis=0)
+    summed = summed.astype(jnp.bfloat16).reshape(experts_here, tile_rows, -1)
     returned = lax.all_to_all(summed, "eg", 0, 0, tiled=True)
     returned = returned.reshape(slot_count, 2 * model_width).astype(jnp.float32)
     expert_out = returned[:, :model_width]

time: 287 us -> 227 us (0.79)
  the two profiles are of different devices: /device:TPU:128 before, /device:TPU:134 now
where the time goes in v2:
time: 227 us
  blocking collectives  109 us (48%)
  waiting for transfers between devices  55.6 us (24%)
  starting transfers between devices  23.6 us (10%)
  matrix products  15.4 us (7%)
  local copies, waits for them, and re-layouts  12.6 us (6%)
  other arithmetic  9.49 us (4%)
    ppermute x1, waiting for transfers between devices, body(): partner_part = lax.ppermute(sent_half, 'pipe', mirror).astype(jnp.float32)  55.6 us
    all_to_all x1, blocking collectives, body(): arrived = lax.all_to_all(payload, 'eg', 0, 0, tiled=True)  42.5 us
    all_to_all x1, blocking collectives, body(): parts = lax.all_to_all(parts, 'es', 0, 0, tiled=True)  33.8 us
    all_to_all x1, blocking collectives, body(): gathered = lax.all_to_all(copies, 'es', 0, 0, tiled=True)  33 us
    all_to_all x1, starting transfers between devices, body(): returned = lax.all_to_all(summed, 'eg', 0, 0, tiled=True)  12.8 us
    ppermute x1, starting transfers between devices, body(): partner_part = lax.ppermute(sent_half, 'pipe', mirror).astype(jnp.float32)  10.8 us
    another operation x3, other arithmetic  4.64 us
  transfers between devices with their start and end apart: 2, of which 1 were waited for; matrix products, arithmetic and copies ran while one was open for 2% of the time, Pallas kernels for 0%

profile of v2, /device:TPU:134, one launch (start us, length us, event | category | flops | bytes accessed | tf_op | source)
XLA Modules:
  0.0 226.8 jit_solution(3587236245120280311)
XLA Ops:
  0.6 0.9 copy.34
  1.7 4.5 %reduce-window.6 = s32[16,8,128]{2,1,0:T(8,128)S(1)} reduce-window(s32[16,8,128]{2,1,0:T(8,128)S(1)} %fusion.27, s32[]{:T(128)} %constant.7.clone.1), window={size=1x1x128 pad=0_0x0_0x127_0}, to_apply=%region_0.0 | reduce-window | flops 2080768 | bytes 131076 | tf_op jit(solution)/shard_map/reduce-window
  6.8 0.7 add_select_fusion.1
  7.6 0.8 copy.40
  8.7 1.3 convolution_convert_fusion.4
  10.1 2.1 multiply_convert_fusion
  12.3 0.8 reshape.84
  13.0 42.5 %all_to_all.20 = bf16[16,16,1280]{2,1,0:T(8,128)(2,1)S(1)} all-to-all(bf16[16,16,1280]{2,1,0:T(8,128)(2,1)S(1)} %reshape.84), channel_id=1, replica_groups=mesh['pipe'=8,'eg'=16,'es'=4] {'eg'}, dimensions={0} | all-to-all | bytes 1310720 | tf_op jit(solution)/shard_map/all_to_all | solution.py:81
  55.7 33.0 %all_to_all.21 = bf16[64,16,1280]{2,1,0:T(8,128)(2,1)S(1)} all-to-all(bf16[64,16,1280]{2,1,0:T(8,128)(2,1)S(1)} %bitcast.53), channel_id=1, replica_groups=mesh['pipe'=8,'eg'=16,'es'=4] {'es'}, dimensions={0} | all-to-all | bytes 5242880 | tf_op jit(solution)/shard_map/all_to_all | solution.py:85
  88.7 4.0 %reshape.86 = bf16[320,4096]{1,0:T(8,128)(2,1)} reshape(bf16[64,16,1280]{2,1,0:T(8,128)(2,1)S(1)} %all_to_all.21) | data formatting | bytes 5242880 | tf_op jit(solution)/shard_map/reshape | solution.py:86
  92.7 2.3 %fusion.6 = f32[320,192]{0,1:T(8,128)S(1)} fusion(bf16[320,4096]{1,0:T(8,128)(2,1)} %reshape.86, bf16[1,2048,192]{1,2,0:T(8,128)(2,1)} %param.11), kind=kOutput, calls=%fused_computation.13 | convolution fusion | flops 251658240 | bytes 2342912 | tf_op jit(solution)/shard_map/dot_general | solution.py:26
  95.1 1.8 fusion.2
  100.6 33.8 %all_to_all.22 = bf16[4,80,4096]{2,1,0:T(8,128)(2,1)S(1)} all-to-all(bf16[4,80,4096]{2,1,0:T(8,128)(2,1)S(1)} %bitcast.52), channel_id=1, replica_groups=mesh['pipe'=8,'eg'=16,'es'=4] {'es'}, dimensions={0} | all-to-all | bytes 5242880 | tf_op jit(solution)/shard_map/all_to_all | solution.py:94
  134.4 1.4 reduce_sum.44
  135.8 2.7 %reshape.88 = bf16[16,16,1280]{2,1,0:T(8,128)(2,1)} reshape(bf16[80,4096]{1,0:T(8,128)(2,1)} %reduce_sum.44) | data formatting | bytes 1310720 | tf_op jit(solution)/shard_map/reshape | solution.py:96
  138.5 12.8 %all-to-all-start.3 = ((bf16[16,16,1280]{2,1,0:T(8,128)(2,1)}), bf16[16,16,1280]{2,1,0:T(8,128)(2,1)S(1)}, u32[]{:S(2)}, u32[]{:S(2)}) async-start(bf16[16,16,1280]{2,1,0:T(8,128)(2,1)} %reshape.88), calls=%async_computation.3 | async-start | bytes 1310720 | tf_op jit(solution)/shard_map/all_to_all | solution.py:97
  151.4 1.9 convolution_convert_fusion.1
  153.3 0.8 broadcast_select_fusion
  154.1 10.8 %collective-permute-start = (bf16[192,1024]{1,0:T(8,128)(2,1)}, bf16[192,1024]{1,0:T(8,128)(2,1)S(1)}, u32[]{:S(2)}, u32[]{:S(2)}) collective-permute-start(bf16[192,1024]{1,0:T(8,128)(2,1)} %broadcast_select_fusion), channel_id=1, source_target_pairs={{0,448},{64,384},{128,320},{192,256},{256,192},{320,128},{384,64},... | collective-permute-start | bytes 1179656 | tf_op jit(solution)/shard_map/ppermute | solution.py:117
  165.0 55.6 %collective-permute-done = bf16[192,1024]{1,0:T(8,128)(2,1)S(1)} collective-permute-done((bf16[192,1024]{1,0:T(8,128)(2,1)}, bf16[192,1024]{1,0:T(8,128)(2,1)S(1)}, u32[]{:S(2)}, u32[]{:S(2)}) %collective-permute-start) | collective-permute-done | bytes 393248 | tf_op jit(solution)/shard_map/ppermute | solution.py:117
  220.6 0.9 fusion.17
  221.5 0.8 reshape.89
  222.3 1.4 convolution_convert_fusion.2
  223.7 1.9 convolution_convert_fusion.3
  (42 shorter events, 6.4 us)
Async XLA Ops:
  0.6 96.3 %copy-start = (bf16[1,2048,192]{1,2,0:T(8,128)(2,1)S(1)}, bf16[1,2048,192]{1,2,0:T(8,128)(2,1)}, u32[]{:S(2)}) copy-start(bf16[1,2048,192]{1,2,0:T(8,128)(2,1)} %param.12) | copy-start | bytes 2359300
  92.7 2.4 %copy-start.1 = (bf16[320,4096]{1,0:T(8,128)(2,1)S(1)}, bf16[320,4096]{1,0:T(8,128)(2,1)}, u32[]{:S(2)}) copy-start(bf16[320,4096]{1,0:T(8,128)(2,1)} %reshape.86) | copy-start | bytes 7864324
  96.9 1.1 copy-start.3
  97.6 1.6 copy-start.5
  98.6 1.1 copy-start.4
  135.8 15.6 %copy-start.6 = (bf16[320,192]{0,1:T(8,128)(2,1)S(1)}, bf16[320,192]{0,1:T(8,128)(2,1)}, u32[]{:S(2)}) copy-start(bf16[320,192]{0,1:T(8,128)(2,1)} %copy-done.5) | copy-start | bytes 368644
  138.5 83.0 %all-to-all-start.3 = ((bf16[16,16,1280]{2,1,0:T(8,128)(2,1)}), bf16[16,16,1280]{2,1,0:T(8,128)(2,1)S(1)}, u32[]{:S(2)}, u32[]{:S(2)}) async-start(bf16[16,16,1280]{2,1,0:T(8,128)(2,1)} %reshape.88), calls=%async_computation.3 | async-start | bytes 1310720 | tf_op jit(solution)/shard_map/all_to_all | solution.py:97
  154.1 71.5 %copy-start.2 = (f32[80,2048]{1,0:T(8,128)S(1)}, f32[80,2048]{1,0:T(8,128)}, u32[]{:S(2)}) copy-start(f32[80,2048]{1,0:T(8,128)} %get-tuple-element.5) | copy-start | bytes 1966084
  154.1 66.5 %collective-permute-start = (bf16[192,1024]{1,0:T(8,128)(2,1)}, bf16[192,1024]{1,0:T(8,128)(2,1)S(1)}, u32[]{:S(2)}, u32[]{:S(2)}) collective-permute-start(bf16[192,1024]{1,0:T(8,128)(2,1)} %broadcast_select_fusion), channel_id=1, source_target_pairs={{0,448},{64,384},{128,320},{192,256},{256,192},{320,128},{384,64},... | collective-permute-start | bytes 1179656 | tf_op jit(solution)/shard_map/ppermute | solution.py:117

commit v3 on v2

--- a/solution.py
+++ b/solution.py
@@ -3,17 +3,8 @@
 from jax import lax
 from jax.sharding import Mesh, PartitionSpec as P
 
+
 WS = 4
-
-
-def from_partner(block, axis, stride):
-    count = lax.axis_size(axis)
-    route = []
-    for low in range(count):
-        high = low | 1 << stride
-        if high != low and high < count:
-            route += [(low, high), (high, low)]
-    return lax.ppermute(block, axis, route)
 
 
 def silu_parts(preact):
@@ -48,7 +39,7 @@
     return (kept_half, sent_half)
 
 
-def body(tokens, cotangent, expert_ids, gates, w_gate, w_up, w_down):
+def layer(tokens, cotangent, expert_ids, gates, w_gate, w_up, w_down):
     highest = lax.Precision.HIGHEST
     tok_count, model_width = tokens.shape
     chosen_count = expert_ids.shape[1]
@@ -114,7 +105,8 @@
     section_pos = lax.axis_index("pipe")
     kept_half, sent_half = split_half(local_down, section_pos >= sections // 2)
     mirror = [(p, sections - 1 - p) for p in range(sections)]
-    partner_part = lax.ppermute(sent_half, "pipe", mirror).astype(jnp.float32)
+    partner_part = lax.ppermute(sent_half, "pipe", mirror)
+    partner_part = partner_part.astype(jnp.float32)
     down_grad = (kept_half.astype(jnp.float32) + partner_part).astype(jnp.bfloat16)[None]
     return (mixed_out, token_grad, gate_grad, down_grad)
 
@@ -135,7 +127,7 @@
         P("pipe", ("eg", "es"), None),
     )
     return jax.shard_map(
-        body,
+        layer,
         mesh=split,
         in_specs=placed,
         out_specs=(rows, rows, rows, P("pipe", ("eg", "es"), None)),

time: 227 us -> 227 us (level)
  no operation moved by 1% of the time
where the time goes in v3:
time: 227 us
  blocking collectives  109 us (48%)
  waiting for transfers between devices  55.6 us (24%)
  starting transfers between devices  23.6 us (10%)
  matrix products  15.4 us (7%)
  local copies, waits for them, and re-layouts  12.6 us (6%)
  other arithmetic  9.49 us (4%)
    ppermute x1, waiting for transfers between devices, layer(): partner_part = lax.ppermute(sent_half, 'pipe', mirror)  55.6 us
    all_to_all x1, blocking collectives, layer(): arrived = lax.all_to_all(payload, 'eg', 0, 0, tiled=True)  42.5 us
    all_to_all x1, blocking collectives, layer(): parts = lax.all_to_all(parts, 'es', 0, 0, tiled=True)  33.8 us
    all_to_all x1, blocking collectives, layer(): gathered = lax.all_to_all(copies, 'es', 0, 0, tiled=True)  33 us
    all_to_all x1, starting transfers between devices, layer(): returned = lax.all_to_all(summed, 'eg', 0, 0, tiled=True)  12.8 us
    ppermute x1, starting transfers between devices, layer(): partner_part = lax.ppermute(sent_half, 'pipe', mirror)  10.8 us
    another operation x3, other arithmetic  4.64 us
  transfers between devices with their start and end apart: 2, of which 1 were waited for; matrix products, arithmetic and copies ran while one was open for 2% of the time, Pallas kernels for 0%

profile of v3, /device:TPU:134, one launch (start us, length us, event | category | flops | bytes accessed | tf_op | source)
XLA Modules:
  0.0 226.8 jit_solution(3587236245120280311)
XLA Ops:
  0.6 0.9 copy.34
  1.7 4.5 %reduce-window.6 = s32[16,8,128]{2,1,0:T(8,128)S(1)} reduce-window(s32[16,8,128]{2,1,0:T(8,128)S(1)} %fusion.27, s32[]{:T(128)} %constant.7.clone.1), window={size=1x1x128 pad=0_0x0_0x127_0}, to_apply=%region_0.0 | reduce-window | flops 2080768 | bytes 131076 | tf_op jit(solution)/shard_map/reduce-window
  6.8 0.7 add_select_fusion.1
  7.6 0.8 copy.40
  8.7 1.3 convolution_convert_fusion.4
  10.1 2.1 multiply_convert_fusion
  12.3 0.8 reshape.84
  13.0 42.5 %all_to_all.20 = bf16[16,16,1280]{2,1,0:T(8,128)(2,1)S(1)} all-to-all(bf16[16,16,1280]{2,1,0:T(8,128)(2,1)S(1)} %reshape.84), channel_id=1, replica_groups=mesh['pipe'=8,'eg'=16,'es'=4] {'eg'}, dimensions={0} | all-to-all | bytes 1310720 | tf_op jit(solution)/shard_map/all_to_all | solution.py:72
  55.7 33.0 %all_to_all.21 = bf16[64,16,1280]{2,1,0:T(8,128)(2,1)S(1)} all-to-all(bf16[64,16,1280]{2,1,0:T(8,128)(2,1)S(1)} %bitcast.53), channel_id=1, replica_groups=mesh['pipe'=8,'eg'=16,'es'=4] {'es'}, dimensions={0} | all-to-all | bytes 5242880 | tf_op jit(solution)/shard_map/all_to_all | solution.py:76
  88.7 4.0 %reshape.86 = bf16[320,4096]{1,0:T(8,128)(2,1)} reshape(bf16[64,16,1280]{2,1,0:T(8,128)(2,1)S(1)} %all_to_all.21) | data formatting | bytes 5242880 | tf_op jit(solution)/shard_map/reshape | solution.py:77
  92.7 2.3 %fusion.6 = f32[320,192]{0,1:T(8,128)S(1)} fusion(bf16[320,4096]{1,0:T(8,128)(2,1)} %reshape.86, bf16[1,2048,192]{1,2,0:T(8,128)(2,1)} %param.11), kind=kOutput, calls=%fused_computation.13 | convolution fusion | flops 251658240 | bytes 2342912 | tf_op jit(solution)/shard_map/dot_general | solution.py:17
  95.1 1.8 fusion.2
  100.6 33.8 %all_to_all.22 = bf16[4,80,4096]{2,1,0:T(8,128)(2,1)S(1)} all-to-all(bf16[4,80,4096]{2,1,0:T(8,128)(2,1)S(1)} %bitcast.52), channel_id=1, replica_groups=mesh['pipe'=8,'eg'=16,'es'=4] {'es'}, dimensions={0} | all-to-all | bytes 5242880 | tf_op jit(solution)/shard_map/all_to_all | solution.py:85
  134.4 1.4 reduce_sum.44
  135.8 2.7 %reshape.88 = bf16[16,16,1280]{2,1,0:T(8,128)(2,1)} reshape(bf16[80,4096]{1,0:T(8,128)(2,1)} %reduce_sum.44) | data formatting | bytes 1310720 | tf_op jit(solution)/shard_map/reshape | solution.py:87
  138.5 12.8 %all-to-all-start.3 = ((bf16[16,16,1280]{2,1,0:T(8,128)(2,1)}), bf16[16,16,1280]{2,1,0:T(8,128)(2,1)S(1)}, u32[]{:S(2)}, u32[]{:S(2)}) async-start(bf16[16,16,1280]{2,1,0:T(8,128)(2,1)} %reshape.88), calls=%async_computation.3 | async-start | bytes 1310720 | tf_op jit(solution)/shard_map/all_to_all | solution.py:88
  151.4 1.9 convolution_convert_fusion.1
  153.3 0.8 broadcast_select_fusion
  154.1 10.8 %collective-permute-start = (bf16[192,1024]{1,0:T(8,128)(2,1)}, bf16[192,1024]{1,0:T(8,128)(2,1)S(1)}, u32[]{:S(2)}, u32[]{:S(2)}) collective-permute-start(bf16[192,1024]{1,0:T(8,128)(2,1)} %broadcast_select_fusion), channel_id=1, source_target_pairs={{0,448},{64,384},{128,320},{192,256},{256,192},{320,128},{384,64},... | collective-permute-start | bytes 1179656 | tf_op jit(solution)/shard_map/ppermute | solution.py:108
  165.0 55.6 %collective-permute-done = bf16[192,1024]{1,0:T(8,128)(2,1)S(1)} collective-permute-done((bf16[192,1024]{1,0:T(8,128)(2,1)}, bf16[192,1024]{1,0:T(8,128)(2,1)S(1)}, u32[]{:S(2)}, u32[]{:S(2)}) %collective-permute-start) | collective-permute-done | bytes 393248 | tf_op jit(solution)/shard_map/ppermute | solution.py:108
  220.6 0.9 fusion.17
  221.5 0.8 reshape.89
  222.3 1.4 convolution_convert_fusion.2
  223.7 1.9 convolution_convert_fusion.3
  (42 shorter events, 6.4 us)
Async XLA Ops:
  0.6 96.3 %copy-start = (bf16[1,2048,192]{1,2,0:T(8,128)(2,1)S(1)}, bf16[1,2048,192]{1,2,0:T(8,128)(2,1)}, u32[]{:S(2)}) copy-start(bf16[1,2048,192]{1,2,0:T(8,128)(2,1)} %param.12) | copy-start | bytes 2359300
  92.7 2.4 %copy-start.1 = (bf16[320,4096]{1,0:T(8,128)(2,1)S(1)}, bf16[320,4096]{1,0:T(8,128)(2,1)}, u32[]{:S(2)}) copy-start(bf16[320,4096]{1,0:T(8,128)(2,1)} %reshape.86) | copy-start | bytes 7864324
  96.9 1.1 copy-start.3
  97.6 1.6 copy-start.5
  98.6 1.1 copy-start.4
  135.8 15.6 %copy-start.6 = (bf16[320,192]{0,1:T(8,128)(2,1)S(1)}, bf16[320,192]{0,1:T(8,128)(2,1)}, u32[]{:S(2)}) copy-start(bf16[320,192]{0,1:T(8,128)(2,1)} %copy-done.5) | copy-start | bytes 368644
  138.5 83.0 %all-to-all-start.3 = ((bf16[16,16,1280]{2,1,0:T(8,128)(2,1)}), bf16[16,16,1280]{2,1,0:T(8,128)(2,1)S(1)}, u32[]{:S(2)}, u32[]{:S(2)}) async-start(bf16[16,16,1280]{2,1,0:T(8,128)(2,1)} %reshape.88), calls=%async_computation.3 | async-start | bytes 1310720 | tf_op jit(solution)/shard_map/all_to_all | solution.py:88
  154.1 71.5 %copy-start.2 = (f32[80,2048]{1,0:T(8,128)S(1)}, f32[80,2048]{1,0:T(8,128)}, u32[]{:S(2)}) copy-start(f32[80,2048]{1,0:T(8,128)} %get-tuple-element.5) | copy-start | bytes 1966084
  154.1 66.5 %collective-permute-start = (bf16[192,1024]{1,0:T(8,128)(2,1)}, bf16[192,1024]{1,0:T(8,128)(2,1)S(1)}, u32[]{:S(2)}, u32[]{:S(2)}) collective-permute-start(bf16[192,1024]{1,0:T(8,128)(2,1)} %broadcast_select_fusion), channel_id=1, source_target_pairs={{0,448},{64,384},{128,320},{192,256},{256,192},{320,128},{384,64},... | collective-permute-start | bytes 1179656 | tf_op jit(solution)/shard_map/ppermute | solution.py:108

commit v4 on v3

--- a/solution.py
+++ b/solution.py
@@ -42,22 +42,21 @@
 def layer(tokens, cotangent, expert_ids, gates, w_gate, w_up, w_down):
     highest = lax.Precision.HIGHEST
     tok_count, model_width = tokens.shape
-    chosen_count = expert_ids.shape[1]
     experts_here = lax.axis_size("eg")
     shards = lax.axis_size("es")
     capacity = tok_count // 24
     slot_count = experts_here * capacity
-    flat_ids = expert_ids.reshape(-1)
     window_ids = jnp.arange(experts_here, dtype=jnp.int32)
-    onehot = (flat_ids[:, None] == window_ids[None, :]).astype(jnp.int32)
-    earlier = jnp.cumsum(onehot, axis=0) - onehot
-    slot_rank = jnp.sum(earlier * onehot, axis=1)
-    in_window = (flat_ids < experts_here) & (slot_rank < capacity)
-    target_slot = jnp.where(in_window, flat_ids * capacity + slot_rank, slot_count)
-    slot_numbers = jnp.arange(slot_count, dtype=jnp.int32)
-    pick_pair = (target_slot[None, :] == slot_numbers[:, None]).astype(jnp.float32)
-    pick_token = pick_pair.reshape(slot_count, tok_count, chosen_count).sum(axis=2)
-    slot_gate = jnp.dot(pick_pair, gates.reshape(-1), precision=highest)
+    named = expert_ids[:, :, None] == window_ids[None, None, :]
+    present = jnp.any(named, axis=1).astype(jnp.float32)
+    token_pos = jnp.arange(tok_count, dtype=jnp.int32)
+    before = (token_pos[None, :] < token_pos[:, None]).astype(jnp.float32)
+    prefix = jnp.dot(before, present, precision=highest)
+    ranks = jnp.arange(capacity, dtype=jnp.float32)
+    pick_block = present.T[:, None, :] * (prefix.T[:, None, :] == ranks[None, :, None])
+    pick_token = pick_block.reshape(slot_count, tok_count)
+    gate_te = jnp.sum(jnp.where(named, gates[:, :, None], 0.0), axis=1)
+    slot_gate = jnp.sum(pick_block * gate_te.T[:, None, :], axis=2).reshape(slot_count)
     pick_narrow = pick_token.astype(jnp.bfloat16)
     slot_rows = jnp.dot(pick_narrow, tokens, preferred_element_type=jnp.float32).astype(
         jnp.bfloat16
@@ -93,7 +92,8 @@
     weighted = slot_gate[:, None] * expert_out
     mixed_out = jnp.dot(pick_token.T, weighted, precision=highest).astype(jnp.bfloat16)
     slot_value = jnp.sum(slot_cot * expert_out, axis=1)
-    gate_grad = jnp.dot(slot_value, pick_pair, precision=highest).reshape(tok_count, chosen_count)
+    value_te = jnp.sum(pick_block * slot_value.reshape(experts_here, capacity, 1), axis=1)
+    gate_grad = jnp.sum(jnp.where(named, value_te.T[:, None, :], 0.0), axis=2)
     token_grad = jnp.dot(pick_token.T, grad_terms, precision=highest).astype(jnp.bfloat16)
     local_down = lax.dot_general(
         hidden,

time: 227 us -> 222 us (0.978)
  other arithmetic: 9.49 us -> 5.28 us
    another operation x3 -> x0, other arithmetic: 4.64 us -> none
  transfers between devices with their start and end apart: 2 -> 2, of which waited for: 1 -> 1; matrix products, arithmetic and copies ran while one was open for 2% -> 1% of each run, Pallas kernels for 0% -> 0%
where the time goes in v4:
time: 222 us
  blocking collectives  109 us (49%)
  waiting for transfers between devices  56.8 us (26%)
  starting transfers between devices  23.6 us (11%)
  matrix products  14.8 us (7%)
  local copies, waits for them, and re-layouts  11 us (5%)
  other arithmetic  5.28 us (2%)
    ppermute x1, waiting for transfers between devices, layer(): partner_part = lax.ppermute(sent_half, 'pipe', mirror)  56.8 us
    all_to_all x1, blocking collectives, layer(): arrived = lax.all_to_all(payload, 'eg', 0, 0, tiled=True)  42.5 us
    all_to_all x1, blocking collectives, layer(): parts = lax.all_to_all(parts, 'es', 0, 0, tiled=True)  33.8 us
    all_to_all x1, blocking collectives, layer(): gathered = lax.all_to_all(copies, 'es', 0, 0, tiled=True)  33 us
    all_to_all x1, starting transfers between devices, layer(): returned = lax.all_to_all(summed, 'eg', 0, 0, tiled=True)  12.8 us
    ppermute x1, starting transfers between devices, layer(): partner_part = lax.ppermute(sent_half, 'pipe', mirror)  10.8 us
  transfers between devices with their start and end apart: 2, of which 1 were waited for; matrix products, arithmetic and copies ran while one was open for 1% of the time, Pallas kernels for 0%

profile of v4, /device:TPU:134, one launch (start us, length us, event | category | flops | bytes accessed | tf_op | source)
XLA Modules:
  0.0 221.7 jit_solution(18162275823437290212)
XLA Ops:
  0.6 0.8 fusion.24
  1.7 0.7 select_reduce_fusion.1
  2.7 1.3 convolution_convert_fusion.4
  4.0 2.1 multiply_convert_fusion
  6.2 0.8 reshape.40
  7.0 42.5 %all_to_all.20 = bf16[16,16,1280]{2,1,0:T(8,128)(2,1)S(1)} all-to-all(bf16[16,16,1280]{2,1,0:T(8,128)(2,1)S(1)} %reshape.40), channel_id=1, replica_groups=mesh['pipe'=8,'eg'=16,'es'=4] {'eg'}, dimensions={0} | all-to-all | bytes 1310720 | tf_op jit(solution)/shard_map/all_to_all | solution.py:71
  49.7 33.0 %all_to_all.21 = bf16[64,16,1280]{2,1,0:T(8,128)(2,1)S(1)} all-to-all(bf16[64,16,1280]{2,1,0:T(8,128)(2,1)S(1)} %bitcast.33), channel_id=1, replica_groups=mesh['pipe'=8,'eg'=16,'es'=4] {'es'}, dimensions={0} | all-to-all | bytes 5242880 | tf_op jit(solution)/shard_map/all_to_all | solution.py:75
  82.7 4.0 %reshape.42 = bf16[320,4096]{1,0:T(8,128)(2,1)} reshape(bf16[64,16,1280]{2,1,0:T(8,128)(2,1)S(1)} %all_to_all.21) | data formatting | bytes 5242880 | tf_op jit(solution)/shard_map/reshape | solution.py:76
  86.7 2.3 %fusion.6 = f32[320,192]{0,1:T(8,128)S(1)} fusion(bf16[320,4096]{1,0:T(8,128)(2,1)} %reshape.42, bf16[1,2048,192]{1,2,0:T(8,128)(2,1)} %param.11), kind=kOutput, calls=%fused_computation.13 | convolution fusion | flops 251658240 | bytes 2342912 | tf_op jit(solution)/shard_map/dot_general | solution.py:17
  89.0 1.8 fusion.2
  90.9 0.7 multiply_convert_fusion.3
  92.0 0.6 fusion.12
  94.5 33.8 %all_to_all.22 = bf16[4,80,4096]{2,1,0:T(8,128)(2,1)S(1)} all-to-all(bf16[4,80,4096]{2,1,0:T(8,128)(2,1)S(1)} %bitcast.32), channel_id=1, replica_groups=mesh['pipe'=8,'eg'=16,'es'=4] {'es'}, dimensions={0} | all-to-all | bytes 5242880 | tf_op jit(solution)/shard_map/all_to_all | solution.py:84
  128.3 1.4 reduce_sum.59
  129.7 2.8 %reshape.44 = bf16[16,16,1280]{2,1,0:T(8,128)(2,1)} reshape(bf16[80,4096]{1,0:T(8,128)(2,1)} %reduce_sum.59) | data formatting | bytes 1310720 | tf_op jit(solution)/shard_map/reshape | solution.py:86
  132.6 12.8 %all-to-all-start.3 = ((bf16[16,16,1280]{2,1,0:T(8,128)(2,1)}), bf16[16,16,1280]{2,1,0:T(8,128)(2,1)}, u32[]{:S(2)}, u32[]{:S(2)}) async-start(bf16[16,16,1280]{2,1,0:T(8,128)(2,1)} %reshape.44), calls=%async_computation.3 | async-start | bytes 1310720 | tf_op jit(solution)/shard_map/all_to_all | solution.py:87
  145.4 1.5 convolution_convert_fusion.1
  147.0 10.8 %collective-permute-start = (bf16[192,1024]{1,0:T(8,128)(2,1)S(1)}, bf16[192,1024]{1,0:T(8,128)(2,1)S(1)}, u32[]{:S(2)}, u32[]{:S(2)}) collective-permute-start(bf16[192,1024]{1,0:T(8,128)(2,1)S(1)} %broadcast_select_fusion), channel_id=1, source_target_pairs={{0,448},{64,384},{128,320},{192,256},{256,192},{320,128},{384,64},... | collective-permute-start | bytes 1179656 | tf_op jit(solution)/shard_map/ppermute | solution.py:108
  157.8 56.8 %collective-permute-done = bf16[192,1024]{1,0:T(8,128)(2,1)S(1)} collective-permute-done((bf16[192,1024]{1,0:T(8,128)(2,1)S(1)}, bf16[192,1024]{1,0:T(8,128)(2,1)S(1)}, u32[]{:S(2)}, u32[]{:S(2)}) %collective-permute-start) | collective-permute-done | bytes 393248 | tf_op jit(solution)/shard_map/ppermute | solution.py:108
  214.6 0.9 fusion.16
  215.6 1.9 reshape.45
  217.4 1.4 convolution_convert_fusion.2
  218.8 1.9 convolution_convert_fusion.3
  221.1 0.6 select_reduce_fusion
  (37 shorter events, 3.6 us)
Async XLA Ops:
  0.6 90.2 %copy-start = (bf16[1,2048,192]{1,2,0:T(8,128)(2,1)S(1)}, bf16[1,2048,192]{1,2,0:T(8,128)(2,1)}, u32[]{:S(2)}) copy-start(bf16[1,2048,192]{1,2,0:T(8,128)(2,1)} %param.12) | copy-start | bytes 2359300
  86.7 2.4 %copy-start.1 = (bf16[320,4096]{1,0:T(8,128)(2,1)S(1)}, bf16[320,4096]{1,0:T(8,128)(2,1)}, u32[]{:S(2)}) copy-start(bf16[320,4096]{1,0:T(8,128)(2,1)} %reshape.42) | copy-start | bytes 7864324
  90.8 1.1 copy-start.4
  91.6 1.6 copy-start.6
  92.6 1.1 copy-start.5
  129.7 15.7 %copy-start.2 = (bf16[320,4096]{1,0:T(8,128)(2,1)S(1)}, bf16[320,4096]{1,0:T(8,128)(2,1)}, u32[]{:S(2)}) copy-start(bf16[320,4096]{1,0:T(8,128)(2,1)} %reshape.42) | copy-start | bytes 7864324
  132.6 83.0 %all-to-all-start.3 = ((bf16[16,16,1280]{2,1,0:T(8,128)(2,1)}), bf16[16,16,1280]{2,1,0:T(8,128)(2,1)}, u32[]{:S(2)}, u32[]{:S(2)}) async-start(bf16[16,16,1280]{2,1,0:T(8,128)(2,1)} %reshape.44), calls=%async_computation.3 | async-start | bytes 1310720 | tf_op jit(solution)/shard_map/all_to_all | solution.py:87
  147.0 73.7 %copy-start.3 = (f32[80,2048]{1,0:T(8,128)S(1)}, f32[80,2048]{1,0:T(8,128)}, u32[]{:S(2)}) copy-start(f32[80,2048]{1,0:T(8,128)} %get-tuple-element.5) | copy-start | bytes 1966084
  147.0 74.1 %copy-start.7 = (s32[128,8]{0,1:T(8,128)S(1)}, s32[128,8]{0,1:T(8,128)}, u32[]{:S(2)}) copy-start(s32[128,8]{0,1:T(8,128)} %param.9) | copy-start | bytes 12292
  147.0 67.6 %collective-permute-start = (bf16[192,1024]{1,0:T(8,128)(2,1)S(1)}, bf16[192,1024]{1,0:T(8,128)(2,1)S(1)}, u32[]{:S(2)}, u32[]{:S(2)}) collective-permute-start(bf16[192,1024]{1,0:T(8,128)(2,1)S(1)} %broadcast_select_fusion), channel_id=1, source_target_pairs={{0,448},{64,384},{128,320},{192,256},{256,192},{320,128},{384,64},... | collective-permute-start | bytes 1179656 | tf_op jit(solution)/shard_map/ppermute | solution.py:108

commit v5 on v4

--- a/solution.py
+++ b/solution.py
@@ -40,7 +40,6 @@
 
 
 def layer(tokens, cotangent, expert_ids, gates, w_gate, w_up, w_down):
-    highest = lax.Precision.HIGHEST
     tok_count, model_width = tokens.shape
     experts_here = lax.axis_size("eg")
     shards = lax.axis_size("es")
@@ -51,7 +50,7 @@
     present = jnp.any(named, axis=1).astype(jnp.float32)
     token_pos = jnp.arange(tok_count, dtype=jnp.int32)
     before = (token_pos[None, :] < token_pos[:, None]).astype(jnp.float32)
-    prefix = jnp.dot(before, present, precision=highest)
+    prefix = jnp.dot(before, present, preferred_element_type=jnp.float32)
     ranks = jnp.arange(capacity, dtype=jnp.float32)
     pick_block = present.T[:, None, :] * (prefix.T[:, None, :] == ranks[None, :, None])
     pick_token = pick_block.reshape(slot_count, tok_count)
@@ -90,22 +89,28 @@
     grad_terms = returned[:, model_width:]
 
     weighted = slot_gate[:, None] * expert_out
-    mixed_out = jnp.dot(pick_token.T, weighted, precision=highest).astype(jnp.bfloat16)
+    mixed_out = jnp.dot(pick_token.T, weighted, precision=lax.Precision.HIGH)
+    mixed_out = mixed_out.astype(jnp.bfloat16)
     slot_value = jnp.sum(slot_cot * expert_out, axis=1)
     value_te = jnp.sum(pick_block * slot_value.reshape(experts_here, capacity, 1), axis=1)
     gate_grad = jnp.sum(jnp.where(named, value_te.T[:, None, :], 0.0), axis=2)
-    token_grad = jnp.dot(pick_token.T, grad_terms, precision=highest).astype(jnp.bfloat16)
+    token_grad = jnp.dot(pick_token.T, grad_terms, preferred_element_type=jnp.float32)
+    token_grad = token_grad.astype(jnp.bfloat16)
     local_down = lax.dot_general(
         hidden,
         scaled,
         (((0,), (0,)), ((), ())),
         preferred_element_type=jnp.float32,
     ).astype(jnp.bfloat16)
-    sections = lax.axis_size("pipe")
-    section_pos = lax.axis_index("pipe")
-    kept_half, sent_half = split_half(local_down, section_pos >= sections // 2)
-    mirror = [(p, sections - 1 - p) for p in range(sections)]
-    partner_part = lax.ppermute(sent_half, "pipe", mirror)
+    halves = lax.axis_size("zh")
+    rings = lax.axis_size("yy")
+    half_pos = lax.axis_index("zh")
+    ring_pos = lax.axis_index("yy")
+    kept_half, sent_half = split_half(local_down, half_pos >= halves // 2)
+    around = lax.all_gather(sent_half, "yy", axis=0)
+    reflected = lax.dynamic_index_in_dim(around, rings - 1 - ring_pos, 0, keepdims=False)
+    across = lax.all_gather(reflected, "zh", axis=0)
+    partner_part = lax.dynamic_index_in_dim(across, halves - 1 - half_pos, 0, keepdims=False)
     partner_part = partner_part.astype(jnp.float32)
     down_grad = (kept_half.astype(jnp.float32) + partner_part).astype(jnp.bfloat16)[None]
     return (mixed_out, token_grad, gate_grad, down_grad)
@@ -113,23 +118,24 @@
 
 def solution(mesh):
     experts = mesh.shape["expert"]
+    sections = mesh.shape["pipe"]
     split = Mesh(
-        mesh.devices.reshape(mesh.shape["pipe"], experts // WS, WS), ("pipe", "eg", "es")
+        mesh.devices.reshape(2, sections // 2, experts // WS, WS), ("zh", "yy", "eg", "es")
     )
-    rows = P(("pipe", "eg", "es"), None)
+    rows = P(("zh", "yy", "eg", "es"), None)
     placed = (
         rows,
         rows,
         rows,
         rows,
-        P("pipe", None, ("eg", "es")),
-        P("pipe", None, ("eg", "es")),
-        P("pipe", ("eg", "es"), None),
+        P(("zh", "yy"), None, ("eg", "es")),
+        P(("zh", "yy"), None, ("eg", "es")),
+        P(("zh", "yy"), ("eg", "es"), None),
     )
     return jax.shard_map(
         layer,
         mesh=split,
         in_specs=placed,
-        out_specs=(rows, rows, rows, P("pipe", ("eg", "es"), None)),
+        out_specs=(rows, rows, rows, P(("zh", "yy"), ("eg", "es"), None)),
         check_vma=False,
     )

time: 222 us -> 235 us (1.059)
  the two profiles are of different devices: /device:TPU:134 before, /device:TPU:80 now
where the time goes in v5:
time: 235 us; the launch traced here: 234 us
  blocking collectives  143 us (61%)
  waiting for transfers between devices  33 us (14%)
  matrix products  14.6 us (6%)
  between operations  14.3 us (6%)
  local copies, waits for them, and re-layouts  11.7 us (5%)
  starting transfers between devices  10.6 us (5%)
  other arithmetic  7.57 us (3%)
    all_gather x1, blocking collectives, layer(): across = lax.all_gather(reflected, 'zh', axis=0)  60.1 us
    all_to_all x1, blocking collectives, layer(): arrived = lax.all_to_all(payload, 'eg', 0, 0, tiled=True)  48.8 us
    all_to_all x1, blocking collectives, layer(): gathered = lax.all_to_all(copies, 'es', 0, 0, tiled=True)  33.8 us
    all_to_all x1, waiting for transfers between devices, layer(): parts = lax.all_to_all(parts, 'es', 0, 0, tiled=True)  27.5 us
    all_to_all x1, starting transfers between devices, layer(): returned = lax.all_to_all(summed, 'eg', 0, 0, tiled=True)  6.92 us
    all_to_all x1, waiting for transfers between devices, layer(): returned = lax.all_to_all(summed, 'eg', 0, 0, tiled=True)  5.42 us
  transfers between devices with their start and end apart: 3, of which 2 were waited for; matrix products, arithmetic and copies ran while one was open for 4% of the time, Pallas kernels for 0%

profile of v5, /device:TPU:80, one launch (start us, length us, event | category | flops | bytes accessed | tf_op | source)
XLA Modules:
  0.0 234.4 jit_solution(17093617294519994798)
XLA Ops:
  7.2 0.8 fusion.25
  9.3 1.3 convolution_convert_fusion.4
  10.6 2.1 multiply_convert_fusion
  13.5 48.8 %all_to_all.20 = bf16[16,16,1280]{2,1,0:T(8,128)(2,1)S(1)} all-to-all(bf16[16,16,1280]{2,1,0:T(8,128)(2,1)S(1)} %reshape.42), channel_id=1, replica_groups=mesh['zh'=2,'yy'=4,'eg'=16,'es'=4] {'eg'}, dimensions={0} | all-to-all | bytes 1310720 | tf_op jit(solution)/shard_map/all_to_all | solution.py:70
  62.5 33.8 %all_to_all.21 = bf16[64,16,1280]{2,1,0:T(8,128)(2,1)S(1)} all-to-all(bf16[64,16,1280]{2,1,0:T(8,128)(2,1)S(1)} %bitcast.37), channel_id=1, replica_groups=mesh['zh'=2,'yy'=4,'eg'=16,'es'=4] {'es'}, dimensions={0} | all-to-all | bytes 5242880 | tf_op jit(solution)/shard_map/all_to_all | solution.py:74
  96.3 4.0 %reshape.44 = bf16[320,4096]{1,0:T(8,128)(2,1)} reshape(bf16[64,16,1280]{2,1,0:T(8,128)(2,1)S(1)} %all_to_all.21) | data formatting | bytes 5242880 | tf_op jit(solution)/shard_map/reshape | solution.py:75
  100.3 2.3 fusion.6
  102.7 1.8 fusion.2
  107.9 1.8 pad_maximum_fusion
  109.7 3.7 %all-to-all-start.2 = ((bf16[4,80,4096]{2,1,0:T(8,128)(2,1)}), bf16[4,80,4096]{2,1,0:T(8,128)(2,1)S(1)}, u32[]{:S(2)}, u32[]{:S(2)}) async-start(bf16[4,80,4096]{2,1,0:T(8,128)(2,1)} %bitcast.36), calls=%async_computation.2 | async-start | bytes 5242880 | tf_op jit(solution)/shard_map/all_to_all | solution.py:83
  113.4 2.0 convolution_convert_fusion.1
  115.4 0.9 copy-done.1
  116.3 0.8 broadcast_select_fusion
  117.1 27.5 %all-to-all-done.2 = bf16[4,80,4096]{2,1,0:T(8,128)(2,1)S(1)} async-done(((bf16[4,80,4096]{2,1,0:T(8,128)(2,1)}), bf16[4,80,4096]{2,1,0:T(8,128)(2,1)S(1)}, u32[]{:S(2)}, u32[]{:S(2)}) %all-to-all-start.2) | async-done | bytes 2621472 | tf_op jit(solution)/shard_map/all_to_all | solution.py:83
  144.6 1.4 reduce_sum.59
  146.1 2.8 %reshape.46 = bf16[16,16,1280]{2,1,0:T(8,128)(2,1)} reshape(bf16[80,4096]{1,0:T(8,128)(2,1)} %reduce_sum.59) | data formatting | bytes 1310720 | tf_op jit(solution)/shard_map/reshape | solution.py:85
  148.8 6.9 %all-to-all-start.3 = ((bf16[16,16,1280]{2,1,0:T(8,128)(2,1)}), bf16[16,16,1280]{2,1,0:T(8,128)(2,1)S(1)}, u32[]{:S(2)}, u32[]{:S(2)}) async-start(bf16[16,16,1280]{2,1,0:T(8,128)(2,1)} %reshape.46), calls=%async_computation.3 | async-start | bytes 1310720 | tf_op jit(solution)/shard_map/all_to_all | solution.py:86
  155.7 1.0 constant_dynamic-slice_fusion
  156.8 60.1 %all_gather.12 = bf16[2,192,1024]{2,1,0:T(8,128)(2,1)S(1)} all-gather(bf16[1,192,1024]{2,1,0:T(8,128)(2,1)S(1)} %constant_dynamic-slice_fusion), channel_id=1, replica_groups=mesh['zh'=2,'yy'=4,'eg'=16,'es'=4] {'zh'}, dimensions={0}, use_global_device_ids=true | all-gather | bytes 1179648 | tf_op jit(solution)/shard_map/all_gather | solution.py:112
  216.9 0.9 fusion.17
  217.8 5.4 %all-to-all-done.3 = bf16[16,16,1280]{2,1,0:T(8,128)(2,1)S(1)} async-done(((bf16[16,16,1280]{2,1,0:T(8,128)(2,1)}), bf16[16,16,1280]{2,1,0:T(8,128)(2,1)S(1)}, u32[]{:S(2)}, u32[]{:S(2)}) %all-to-all-start.3) | async-done | bytes 655392 | tf_op jit(solution)/shard_map/all_to_all | solution.py:86
  223.2 0.8 reshape.47
  224.0 1.1 convolution_convert_fusion.2
  225.1 1.4 convolution_convert_fusion.3
  (43 shorter events, 6.7 us)
Async XLA Ops:
  7.2 97.3 %copy-start = (bf16[1,2048,192]{1,2,0:T(8,128)(2,1)S(1)}, bf16[1,2048,192]{1,2,0:T(8,128)(2,1)}, u32[]{:S(2)}) copy-start(bf16[1,2048,192]{1,2,0:T(8,128)(2,1)} %param.12) | copy-start | bytes 2359300
  100.3 2.4 %copy-start.3 = (bf16[320,4096]{1,0:T(8,128)(2,1)S(1)}, bf16[320,4096]{1,0:T(8,128)(2,1)}, u32[]{:S(2)}) copy-start(bf16[320,4096]{1,0:T(8,128)(2,1)} %reshape.44) | copy-start | bytes 7864324
  104.5 1.1 copy-start.5
  105.2 1.6 copy-start.7
  106.2 1.1 copy-start.6
  109.7 34.9 %all-to-all-start.2 = ((bf16[4,80,4096]{2,1,0:T(8,128)(2,1)}), bf16[4,80,4096]{2,1,0:T(8,128)(2,1)S(1)}, u32[]{:S(2)}, u32[]{:S(2)}) async-start(bf16[4,80,4096]{2,1,0:T(8,128)(2,1)} %bitcast.36), calls=%async_computation.2 | async-start | bytes 5242880 | tf_op jit(solution)/shard_map/all_to_all | solution.py:83
  113.4 42.4 %all-gather.3.cloned.1.call-start = ((), (), s32[]{:S(2)}) async-start(), calls=%async_computation.4 | async-start | bytes 1966080 | tf_op jit(solution)/shard_map/all_gather | solution.py:110
  115.4 0.9 copy-start.1
  146.0 70.8 %copy-start.2 = (bf16[192,2048]{1,0:T(8,128)(2,1)S(1)}, bf16[192,2048]{1,0:T(8,128)(2,1)}, u32[]{:S(2)}) copy-start(bf16[192,2048]{1,0:T(8,128)(2,1)} %copy-done.1) | copy-start | bytes 2359300
  148.8 74.4 %all-to-all-start.3 = ((bf16[16,16,1280]{2,1,0:T(8,128)(2,1)}), bf16[16,16,1280]{2,1,0:T(8,128)(2,1)S(1)}, u32[]{:S(2)}, u32[]{:S(2)}) async-start(bf16[16,16,1280]{2,1,0:T(8,128)(2,1)} %reshape.46), calls=%async_computation.3 | async-start | bytes 1310720 | tf_op jit(solution)/shard_map/all_to_all | solution.py:86
  216.9 9.7 %copy-start.4 = (f32[80,2048]{1,0:T(8,128)S(1)}, f32[80,2048]{1,0:T(8,128)}, u32[]{:S(2)}) copy-start(f32[80,2048]{1,0:T(8,128)} %get-tuple-element.5) | copy-start | bytes 1966084
  216.9 10.1 %copy-start.8 = (s32[128,8]{0,1:T(8,128)S(1)}, s32[128,8]{0,1:T(8,128)}, u32[]{:S(2)}) copy-start(s32[128,8]{0,1:T(8,128)} %param.9) | copy-start | bytes 12292
Sparse Core Ops, SparseCore 0:
  117.2 30.2 all-gather.2

commit v6 on v4

--- a/solution.py
+++ b/solution.py
@@ -40,7 +40,6 @@
 
 
 def layer(tokens, cotangent, expert_ids, gates, w_gate, w_up, w_down):
-    highest = lax.Precision.HIGHEST
     tok_count, model_width = tokens.shape
     experts_here = lax.axis_size("eg")
     shards = lax.axis_size("es")
@@ -51,7 +50,7 @@
     present = jnp.any(named, axis=1).astype(jnp.float32)
     token_pos = jnp.arange(tok_count, dtype=jnp.int32)
     before = (token_pos[None, :] < token_pos[:, None]).astype(jnp.float32)
-    prefix = jnp.dot(before, present, precision=highest)
+    prefix = jnp.dot(before, present, preferred_element_type=jnp.float32)
     ranks = jnp.arange(capacity, dtype=jnp.float32)
     pick_block = present.T[:, None, :] * (prefix.T[:, None, :] == ranks[None, :, None])
     pick_token = pick_block.reshape(slot_count, tok_count)
@@ -90,11 +89,13 @@
     grad_terms = returned[:, model_width:]
 
     weighted = slot_gate[:, None] * expert_out
-    mixed_out = jnp.dot(pick_token.T, weighted, precision=highest).astype(jnp.bfloat16)
+    mixed_out = jnp.dot(pick_token.T, weighted, precision=lax.Precision.HIGH)
+    mixed_out = mixed_out.astype(jnp.bfloat16)
     slot_value = jnp.sum(slot_cot * expert_out, axis=1)
     value_te = jnp.sum(pick_block * slot_value.reshape(experts_here, capacity, 1), axis=1)
     gate_grad = jnp.sum(jnp.where(named, value_te.T[:, None, :], 0.0), axis=2)
-    token_grad = jnp.dot(pick_token.T, grad_terms, precision=highest).astype(jnp.bfloat16)
+    token_grad = jnp.dot(pick_token.T, grad_terms, preferred_element_type=jnp.float32)
+    token_grad = token_grad.astype(jnp.bfloat16)
     local_down = lax.dot_general(
         hidden,
         scaled,

time: 222 us -> 222 us (level)
  no operation moved by 1% of the time
where the time goes in v6:
time: 222 us; the launch traced here: 221 us
  blocking collectives  109 us (49%)
  waiting for transfers between devices  56.8 us (26%)
  starting transfers between devices  23.6 us (11%)
  matrix products  14.1 us (6%)
  local copies, waits for them, and re-layouts  11 us (5%)
  other arithmetic  5.28 us (2%)
    ppermute x1, waiting for transfers between devices, layer(): partner_part = lax.ppermute(sent_half, 'pipe', mirror)  56.8 us
    all_to_all x1, blocking collectives, layer(): arrived = lax.all_to_all(payload, 'eg', 0, 0, tiled=True)  42.5 us
    all_to_all x1, blocking collectives, layer(): parts = lax.all_to_all(parts, 'es', 0, 0, tiled=True)  33.8 us
    all_to_all x1, blocking collectives, layer(): gathered = lax.all_to_all(copies, 'es', 0, 0, tiled=True)  33 us
    all_to_all x1, starting transfers between devices, layer(): returned = lax.all_to_all(summed, 'eg', 0, 0, tiled=True)  12.8 us
    ppermute x1, starting transfers between devices, layer(): partner_part = lax.ppermute(sent_half, 'pipe', mirror)  10.8 us
  transfers between devices with their start and end apart: 2, of which 1 were waited for; matrix products, arithmetic and copies ran while one was open for 1% of the time, Pallas kernels for 0%

profile of v6, /device:TPU:134, one launch (start us, length us, event | category | flops | bytes accessed | tf_op | source)
XLA Modules:
  0.0 221.0 jit_solution(4343335213414522307)
XLA Ops:
  0.6 0.8 fusion.24
  1.7 0.7 select_reduce_fusion.1
  2.7 1.3 convolution_convert_fusion.4
  4.0 2.1 multiply_convert_fusion
  6.2 0.8 reshape.40
  7.0 42.5 %all_to_all.20 = bf16[16,16,1280]{2,1,0:T(8,128)(2,1)S(1)} all-to-all(bf16[16,16,1280]{2,1,0:T(8,128)(2,1)S(1)} %reshape.40), channel_id=1, replica_groups=mesh['pipe'=8,'eg'=16,'es'=4] {'eg'}, dimensions={0} | all-to-all | bytes 1310720 | tf_op jit(solution)/shard_map/all_to_all | solution.py:70
  49.7 33.0 %all_to_all.21 = bf16[64,16,1280]{2,1,0:T(8,128)(2,1)S(1)} all-to-all(bf16[64,16,1280]{2,1,0:T(8,128)(2,1)S(1)} %bitcast.33), channel_id=1, replica_groups=mesh['pipe'=8,'eg'=16,'es'=4] {'es'}, dimensions={0} | all-to-all | bytes 5242880 | tf_op jit(solution)/shard_map/all_to_all | solution.py:74
  82.7 4.0 %reshape.42 = bf16[320,4096]{1,0:T(8,128)(2,1)} reshape(bf16[64,16,1280]{2,1,0:T(8,128)(2,1)S(1)} %all_to_all.21) | data formatting | bytes 5242880 | tf_op jit(solution)/shard_map/reshape | solution.py:75
  86.7 2.3 %fusion.6 = f32[320,192]{0,1:T(8,128)S(1)} fusion(bf16[320,4096]{1,0:T(8,128)(2,1)} %reshape.42, bf16[1,2048,192]{1,2,0:T(8,128)(2,1)} %param.11), kind=kOutput, calls=%fused_computation.13 | convolution fusion | flops 251658240 | bytes 2342912 | tf_op jit(solution)/shard_map/dot_general | solution.py:17
  89.0 1.8 fusion.2
  90.9 0.7 multiply_convert_fusion.3
  92.0 0.6 fusion.12
  94.5 33.8 %all_to_all.22 = bf16[4,80,4096]{2,1,0:T(8,128)(2,1)S(1)} all-to-all(bf16[4,80,4096]{2,1,0:T(8,128)(2,1)S(1)} %bitcast.32), channel_id=1, replica_groups=mesh['pipe'=8,'eg'=16,'es'=4] {'es'}, dimensions={0} | all-to-all | bytes 5242880 | tf_op jit(solution)/shard_map/all_to_all | solution.py:83
  128.3 1.4 reduce_sum.59
  129.7 2.8 %reshape.44 = bf16[16,16,1280]{2,1,0:T(8,128)(2,1)} reshape(bf16[80,4096]{1,0:T(8,128)(2,1)} %reduce_sum.59) | data formatting | bytes 1310720 | tf_op jit(solution)/shard_map/reshape | solution.py:85
  132.6 12.8 %all-to-all-start.3 = ((bf16[16,16,1280]{2,1,0:T(8,128)(2,1)}), bf16[16,16,1280]{2,1,0:T(8,128)(2,1)}, u32[]{:S(2)}, u32[]{:S(2)}) async-start(bf16[16,16,1280]{2,1,0:T(8,128)(2,1)} %reshape.44), calls=%async_computation.3 | async-start | bytes 1310720 | tf_op jit(solution)/shard_map/all_to_all | solution.py:86
  145.4 1.5 convolution_convert_fusion.1
  147.0 10.8 %collective-permute-start = (bf16[192,1024]{1,0:T(8,128)(2,1)S(1)}, bf16[192,1024]{1,0:T(8,128)(2,1)S(1)}, u32[]{:S(2)}, u32[]{:S(2)}) collective-permute-start(bf16[192,1024]{1,0:T(8,128)(2,1)S(1)} %broadcast_select_fusion), channel_id=1, source_target_pairs={{0,448},{64,384},{128,320},{192,256},{256,192},{320,128},{384,64},... | collective-permute-start | bytes 1179656 | tf_op jit(solution)/shard_map/ppermute | solution.py:109
  157.8 56.8 %collective-permute-done = bf16[192,1024]{1,0:T(8,128)(2,1)S(1)} collective-permute-done((bf16[192,1024]{1,0:T(8,128)(2,1)S(1)}, bf16[192,1024]{1,0:T(8,128)(2,1)S(1)}, u32[]{:S(2)}, u32[]{:S(2)}) %collective-permute-start) | collective-permute-done | bytes 393248 | tf_op jit(solution)/shard_map/ppermute | solution.py:109
  214.6 0.9 fusion.16
  215.6 1.9 reshape.45
  217.4 1.1 convolution_convert_fusion.2
  218.5 1.4 convolution_convert_fusion.3
  220.3 0.6 select_reduce_fusion
  (37 shorter events, 3.6 us)
Async XLA Ops:
  0.6 90.2 %copy-start = (bf16[1,2048,192]{1,2,0:T(8,128)(2,1)S(1)}, bf16[1,2048,192]{1,2,0:T(8,128)(2,1)}, u32[]{:S(2)}) copy-start(bf16[1,2048,192]{1,2,0:T(8,128)(2,1)} %param.12) | copy-start | bytes 2359300
  86.7 2.4 %copy-start.1 = (bf16[320,4096]{1,0:T(8,128)(2,1)S(1)}, bf16[320,4096]{1,0:T(8,128)(2,1)}, u32[]{:S(2)}) copy-start(bf16[320,4096]{1,0:T(8,128)(2,1)} %reshape.42) | copy-start | bytes 7864324
  90.8 1.1 copy-start.4
  91.6 1.6 copy-start.6
  92.6 1.1 copy-start.5
  129.7 15.7 %copy-start.2 = (bf16[320,4096]{1,0:T(8,128)(2,1)S(1)}, bf16[320,4096]{1,0:T(8,128)(2,1)}, u32[]{:S(2)}) copy-start(bf16[320,4096]{1,0:T(8,128)(2,1)} %reshape.42) | copy-start | bytes 7864324
  132.6 83.0 %all-to-all-start.3 = ((bf16[16,16,1280]{2,1,0:T(8,128)(2,1)}), bf16[16,16,1280]{2,1,0:T(8,128)(2,1)}, u32[]{:S(2)}, u32[]{:S(2)}) async-start(bf16[16,16,1280]{2,1,0:T(8,128)(2,1)} %reshape.44), calls=%async_computation.3 | async-start | bytes 1310720 | tf_op jit(solution)/shard_map/all_to_all | solution.py:86
  147.0 73.0 %copy-start.3 = (f32[80,2048]{1,0:T(8,128)S(1)}, f32[80,2048]{1,0:T(8,128)}, u32[]{:S(2)}) copy-start(f32[80,2048]{1,0:T(8,128)} %get-tuple-element.5) | copy-start | bytes 1966084
  147.0 73.3 %copy-start.7 = (s32[128,8]{0,1:T(8,128)S(1)}, s32[128,8]{0,1:T(8,128)}, u32[]{:S(2)}) copy-start(s32[128,8]{0,1:T(8,128)} %param.9) | copy-start | bytes 12292
  147.0 67.6 %collective-permute-start = (bf16[192,1024]{1,0:T(8,128)(2,1)S(1)}, bf16[192,1024]{1,0:T(8,128)(2,1)S(1)}, u32[]{:S(2)}, u32[]{:S(2)}) collective-permute-start(bf16[192,1024]{1,0:T(8,128)(2,1)S(1)} %broadcast_select_fusion), channel_id=1, source_target_pairs={{0,448},{64,384},{128,320},{192,256},{256,192},{320,128},{384,64},... | collective-permute-start | bytes 1179656 | tf_op jit(solution)/shard_map/ppermute | solution.py:109

commit v7 on v6

--- a/solution.py
+++ b/solution.py
@@ -42,7 +42,7 @@
 def layer(tokens, cotangent, expert_ids, gates, w_gate, w_up, w_down):
     tok_count, model_width = tokens.shape
     experts_here = lax.axis_size("eg")
-    shards = lax.axis_size("es")
+    shards = lax.axis_size("xs") * lax.axis_size("core")
     capacity = tok_count // 24
     slot_count = experts_here * capacity
     window_ids = jnp.arange(experts_here, dtype=jnp.int32)
@@ -68,10 +68,14 @@
         experts_here, tile_rows, -1
     )
     arrived = lax.all_to_all(payload, "eg", 0, 0, tiled=True)
-    copies = jnp.broadcast_to(arrived[None], (shards,) + arrived.shape).reshape(
+    pair = jnp.broadcast_to(arrived[None], (2,) + arrived.shape).reshape(
+        (2 * experts_here,) + arrived.shape[1:]
+    )
+    pair = lax.all_to_all(pair, "xs", 0, 0, tiled=True)
+    copies = jnp.broadcast_to(pair[None], (2,) + pair.shape).reshape(
         (shards * experts_here,) + arrived.shape[1:]
     )
-    gathered = lax.all_to_all(copies, "es", 0, 0, tiled=True)
+    gathered = lax.all_to_all(copies, "core", 0, 0, tiled=True)
     gathered = gathered.reshape(shards * experts_here * capacity, 2 * model_width)
     inputs = gathered[:, :model_width]
     scaled = gathered[:, model_width:]
@@ -79,9 +83,12 @@
         inputs, scaled, w_gate[0], w_up[0], w_down[0]
     )
 
-    parts = jnp.concatenate([group_out, group_grad], axis=1).reshape(shards, slot_count, -1)
-    parts = lax.all_to_all(parts, "es", 0, 0, tiled=True)
-    summed = parts.astype(jnp.float32).sum(axis=0)
+    parts = jnp.concatenate([group_out, group_grad], axis=1).reshape(2, 2 * slot_count, -1)
+    parts = lax.all_to_all(parts, "core", 0, 0, tiled=True)
+    on_chip = parts.astype(jnp.float32).sum(axis=0).astype(jnp.bfloat16)
+    on_chip = on_chip.reshape(2, slot_count, -1)
+    across = lax.all_to_all(on_chip, "xs", 0, 0, tiled=True)
+    summed = across.astype(jnp.float32).sum(axis=0)
     summed = summed.astype(jnp.bfloat16).reshape(experts_here, tile_rows, -1)
     returned = lax.all_to_all(summed, "eg", 0, 0, tiled=True)
     returned = returned.reshape(slot_count, 2 * model_width).astype(jnp.float32)
@@ -115,22 +122,24 @@
 def solution(mesh):
     experts = mesh.shape["expert"]
     split = Mesh(
-        mesh.devices.reshape(mesh.shape["pipe"], experts // WS, WS), ("pipe", "eg", "es")
+        mesh.devices.reshape(mesh.shape["pipe"], experts // WS, 2, WS // 2),
+        ("pipe", "eg", "xs", "core"),
     )
-    rows = P(("pipe", "eg", "es"), None)
+    shard = ("eg", "xs", "core")
+    rows = P(("pipe",) + shard, None)
     placed = (
         rows,
         rows,
         rows,
         rows,
-        P("pipe", None, ("eg", "es")),
-        P("pipe", None, ("eg", "es")),
-        P("pipe", ("eg", "es"), None),
+        P("pipe", None, shard),
+        P("pipe", None, shard),
+        P("pipe", shard, None),
     )
     return jax.shard_map(
         layer,
         mesh=split,
         in_specs=placed,
-        out_specs=(rows, rows, rows, P("pipe", ("eg", "es"), None)),
+        out_specs=(rows, rows, rows, P("pipe", shard, None)),
         check_vma=False,
     )

time: 222 us -> 207 us (0.932)
  the two profiles are of different devices: /device:TPU:134 before, /device:TPU:128 now
where the time goes in v7:
time: 207 us; the launch traced here: 206 us
  blocking collectives  95.2 us (46%)
  waiting for transfers between devices  56.2 us (27%)
  starting transfers between devices  21.3 us (10%)
  matrix products  14.1 us (7%)
  local copies, waits for them, and re-layouts  11 us (5%)
  other arithmetic  7.07 us (3%)
    ppermute x1, waiting for transfers between devices, layer(): partner_part = lax.ppermute(sent_half, 'pipe', mirror)  56.2 us
    all_to_all x1, blocking collectives, layer(): arrived = lax.all_to_all(payload, 'eg', 0, 0, tiled=True)  44.6 us
    all_to_all x1, blocking collectives, layer(): across = lax.all_to_all(on_chip, 'xs', 0, 0, tiled=True)  20.6 us
    all_to_all x1, blocking collectives, layer(): pair = lax.all_to_all(pair, 'xs', 0, 0, tiled=True)  18.3 us
    ppermute x1, starting transfers between devices, layer(): partner_part = lax.ppermute(sent_half, 'pipe', mirror)  10.8 us
    all_to_all x1, starting transfers between devices, layer(): returned = lax.all_to_all(summed, 'eg', 0, 0, tiled=True)  10.4 us
    all_to_all x1, blocking collectives, layer(): gathered = lax.all_to_all(copies, 'core', 0, 0, tiled=True)  5.84 us
    all_to_all x1, blocking collectives, layer(): parts = lax.all_to_all(parts, 'core', 0, 0, tiled=True)  5.84 us
  transfers between devices with their start and end apart: 2, of which 1 were waited for; matrix products, arithmetic and copies ran while one was open for 1% of the time, Pallas kernels for 0%

profile of v7, /device:TPU:128, one launch (start us, length us, event | category | flops | bytes accessed | tf_op | source)
XLA Modules:
  0.0 205.7 jit_solution(7004019759535121016)
XLA Ops:
  0.6 0.8 fusion.24
  1.7 0.7 select_reduce_fusion.1
  2.7 1.3 convolution_convert_fusion.4
  4.0 2.1 %multiply_convert_fusion = (bf16[80,2048]{1,0:T(8,128)(2,1)S(1)}, f32[80,2048]{1,0:T(8,128)}) fusion(f32[80]{0:T(128)S(1)} %mul.76, bf16[128,2048]{1,0:T(8,128)(2,1)} %param.8, f32[80,128]{1,0:T(8,128)S(1)} %compare_select_fusion), kind=kOutput, calls=%fused_computation.27 | convolution fusion | flops 42280960 | bytes 1548608 | tf_op jit(solution)/shard_map/dot_general | solution.py:63
  6.2 0.8 reshape.47
  7.0 44.6 %all_to_all.30 = bf16[16,16,1280]{2,1,0:T(8,128)(2,1)S(1)} all-to-all(bf16[16,16,1280]{2,1,0:T(8,128)(2,1)S(1)} %reshape.47), channel_id=1, replica_groups=mesh['pipe'=8,'eg'=16,'xs'=2,'core'=2] {'eg'}, dimensions={0} | all-to-all | bytes 1310720 | tf_op jit(solution)/shard_map/all_to_all | solution.py:70
  51.7 18.3 %all_to_all.31 = bf16[32,16,1280]{2,1,0:T(8,128)(2,1)S(1)} all-to-all(bf16[32,16,1280]{2,1,0:T(8,128)(2,1)S(1)} %bitcast.36), channel_id=1, replica_groups=mesh['pipe'=8,'eg'=16,'xs'=2,'core'=2] {'xs'}, dimensions={0} | all-to-all | bytes 2621440 | tf_op jit(solution)/shard_map/all_to_all | solution.py:74
  70.2 5.8 %all_to_all.32 = bf16[64,16,1280]{2,1,0:T(8,128)(2,1)S(1)} all-to-all(bf16[64,16,1280]{2,1,0:T(8,128)(2,1)S(1)} %bitcast.35), channel_id=1, replica_groups=mesh['pipe'=8,'eg'=16,'xs'=2,'core'=2] {'core'}, dimensions={0} | all-to-all | bytes 5242880 | tf_op jit(solution)/shard_map/all_to_all | solution.py:78
  76.0 4.0 %reshape.50 = bf16[320,4096]{1,0:T(8,128)(2,1)} reshape(bf16[64,16,1280]{2,1,0:T(8,128)(2,1)S(1)} %all_to_all.32) | data formatting | bytes 5242880 | tf_op jit(solution)/shard_map/reshape | solution.py:79
  80.0 2.3 %fusion.6 = f32[320,192]{0,1:T(8,128)S(1)} fusion(bf16[320,4096]{1,0:T(8,128)(2,1)} %reshape.50, bf16[1,2048,192]{1,2,0:T(8,128)(2,1)} %param.11), kind=kOutput, calls=%fused_computation.13 | convolution fusion | flops 251658240 | bytes 2342912 | tf_op jit(solution)/shard_map/dot_general | solution.py:17
  82.4 1.8 fusion.2
  87.9 5.8 %all_to_all.33 = bf16[2,160,4096]{2,1,0:T(8,128)(2,1)S(1)} all-to-all(bf16[2,160,4096]{2,1,0:T(8,128)(2,1)S(1)} %bitcast.34), channel_id=1, replica_groups=mesh['pipe'=8,'eg'=16,'xs'=2,'core'=2] {'core'}, dimensions={0} | all-to-all | bytes 5242880 | tf_op jit(solution)/shard_map/all_to_all | solution.py:87
  93.7 2.0 reduce_sum.71
  95.7 20.6 %all_to_all.34 = bf16[2,80,4096]{2,1,0:T(8,128)(2,1)S(1)} all-to-all(bf16[2,80,4096]{2,1,0:T(8,128)(2,1)} %bitcast.37), channel_id=1, replica_groups=mesh['pipe'=8,'eg'=16,'xs'=2,'core'=2] {'xs'}, dimensions={0} | all-to-all | bytes 2621440 | tf_op jit(solution)/shard_map/all_to_all | solution.py:90
  116.3 1.2 reduce_sum.72
  117.5 2.8 %reshape.53 = bf16[16,16,1280]{2,1,0:T(8,128)(2,1)} reshape(bf16[80,4096]{1,0:T(8,128)(2,1)} %reduce_sum.72) | data formatting | bytes 1310720 | tf_op jit(solution)/shard_map/reshape | solution.py:92
  120.4 10.4 %all-to-all-start.5 = ((bf16[16,16,1280]{2,1,0:T(8,128)(2,1)}), bf16[16,16,1280]{2,1,0:T(8,128)(2,1)}, u32[]{:S(2)}, u32[]{:S(2)}) async-start(bf16[16,16,1280]{2,1,0:T(8,128)(2,1)} %reshape.53), calls=%async_computation.5 | async-start | bytes 1310720 | tf_op jit(solution)/shard_map/all_to_all | solution.py:93
  130.8 1.5 convolution_convert_fusion.1
  132.4 10.8 %collective-permute-start = (bf16[192,1024]{1,0:T(8,128)(2,1)S(1)}, bf16[192,1024]{1,0:T(8,128)(2,1)S(1)}, u32[]{:S(2)}, u32[]{:S(2)}) collective-permute-start(bf16[192,1024]{1,0:T(8,128)(2,1)S(1)} %broadcast_select_fusion), channel_id=1, source_target_pairs={{0,448},{64,384},{128,320},{192,256},{256,192},{320,128},{384,64},... | collective-permute-start | bytes 1179656 | tf_op jit(solution)/shard_map/ppermute | solution.py:116
  143.2 56.2 %collective-permute-done = bf16[192,1024]{1,0:T(8,128)(2,1)S(1)} collective-permute-done((bf16[192,1024]{1,0:T(8,128)(2,1)S(1)}, bf16[192,1024]{1,0:T(8,128)(2,1)S(1)}, u32[]{:S(2)}, u32[]{:S(2)}) %collective-permute-start) | collective-permute-done | bytes 393248 | tf_op jit(solution)/shard_map/ppermute | solution.py:116
  199.4 0.9 fusion.16
  200.4 1.9 reshape.54
  202.2 1.1 convolution_convert_fusion.2
  203.3 1.4 convolution_convert_fusion.3
  (41 shorter events, 5.5 us)
Async XLA Ops:
  0.6 83.6 %copy-start = (bf16[1,2048,192]{1,2,0:T(8,128)(2,1)S(1)}, bf16[1,2048,192]{1,2,0:T(8,128)(2,1)}, u32[]{:S(2)}) copy-start(bf16[1,2048,192]{1,2,0:T(8,128)(2,1)} %param.12) | copy-start | bytes 2359300
  80.0 2.4 %copy-start.1 = (bf16[320,4096]{1,0:T(8,128)(2,1)S(1)}, bf16[320,4096]{1,0:T(8,128)(2,1)}, u32[]{:S(2)}) copy-start(bf16[320,4096]{1,0:T(8,128)(2,1)} %reshape.50) | copy-start | bytes 7864324
  84.2 1.1 copy-start.4
  84.9 1.6 copy-start.6
  85.9 1.1 copy-start.5
  117.5 13.3 %copy-start.2 = (bf16[320,4096]{1,0:T(8,128)(2,1)S(1)}, bf16[320,4096]{1,0:T(8,128)(2,1)}, u32[]{:S(2)}) copy-start(bf16[320,4096]{1,0:T(8,128)(2,1)} %reshape.50) | copy-start | bytes 7864324
  120.4 80.0 %all-to-all-start.5 = ((bf16[16,16,1280]{2,1,0:T(8,128)(2,1)}), bf16[16,16,1280]{2,1,0:T(8,128)(2,1)}, u32[]{:S(2)}, u32[]{:S(2)}) async-start(bf16[16,16,1280]{2,1,0:T(8,128)(2,1)} %reshape.53), calls=%async_computation.5 | async-start | bytes 1310720 | tf_op jit(solution)/shard_map/all_to_all | solution.py:93
  132.4 72.4 %copy-start.3 = (f32[80,2048]{1,0:T(8,128)S(1)}, f32[80,2048]{1,0:T(8,128)}, u32[]{:S(2)}) copy-start(f32[80,2048]{1,0:T(8,128)} %get-tuple-element.5) | copy-start | bytes 1966084
  132.4 72.7 %copy-start.7 = (s32[128,8]{0,1:T(8,128)S(1)}, s32[128,8]{0,1:T(8,128)}, u32[]{:S(2)}) copy-start(s32[128,8]{0,1:T(8,128)} %param.9) | copy-start | bytes 12292
  132.4 67.0 %collective-permute-start = (bf16[192,1024]{1,0:T(8,128)(2,1)S(1)}, bf16[192,1024]{1,0:T(8,128)(2,1)S(1)}, u32[]{:S(2)}, u32[]{:S(2)}) collective-permute-start(bf16[192,1024]{1,0:T(8,128)(2,1)S(1)} %broadcast_select_fusion), channel_id=1, source_target_pairs={{0,448},{64,384},{128,320},{192,256},{256,192},{320,128},{384,64},... | collective-permute-start | bytes 1179656 | tf_op jit(solution)/shard_map/ppermute | solution.py:116

commit v8 on v7

--- a/solution.py
+++ b/solution.py
@@ -72,10 +72,8 @@
         (2 * experts_here,) + arrived.shape[1:]
     )
     pair = lax.all_to_all(pair, "xs", 0, 0, tiled=True)
-    copies = jnp.broadcast_to(pair[None], (2,) + pair.shape).reshape(
-        (shards * experts_here,) + arrived.shape[1:]
-    )
-    gathered = lax.all_to_all(copies, "core", 0, 0, tiled=True)
+    swap = [(0, 1), (1, 0)]
+    gathered = jnp.concatenate([pair, lax.ppermute(pair, "core", swap)])
     gathered = gathered.reshape(shards * experts_here * capacity, 2 * model_width)
     inputs = gathered[:, :model_width]
     scaled = gathered[:, model_width:]
@@ -84,8 +82,8 @@
     )
 
     parts = jnp.concatenate([group_out, group_grad], axis=1).reshape(2, 2 * slot_count, -1)
-    parts = lax.all_to_all(parts, "core", 0, 0, tiled=True)
-    on_chip = parts.astype(jnp.float32).sum(axis=0).astype(jnp.bfloat16)
+    other = lax.ppermute(parts[1], "core", swap)
+    on_chip = (parts[0].astype(jnp.float32) + other.astype(jnp.float32)).astype(jnp.bfloat16)
     on_chip = on_chip.reshape(2, slot_count, -1)
     across = lax.all_to_all(on_chip, "xs", 0, 0, tiled=True)
     summed = across.astype(jnp.float32).sum(axis=0)

time: 207 us -> 201 us (0.971)
  blocking collectives: 95.2 us -> 82.4 us
  waiting for transfers between devices: 56.2 us -> 62.2 us
  starting transfers between devices: 21.3 us -> 25.1 us
    all_to_all x2 -> x0, blocking collectives: 11.7 us -> none  [the longest x1 5.84 us: layer(): gathered = lax.all_to_all(copies, 'core', 0, 0, tiled=True)]
    ppermute x0 -> x2, waiting for transfers between devices: none -> 5.87 us  [the longest x1 3 us: layer(): gathered = jnp.concatenate([pair, lax.ppermute(pair, 'core', swap)])]
    ppermute x0 -> x2, starting transfers between devices: none -> 3.96 us  [the longest x1 2.05 us: layer(): other = lax.ppermute(parts[1], 'core', swap)]
  transfers between devices with their start and end apart: 2 -> 4, of which waited for: 1 -> 3; matrix products, arithmetic and copies ran while one was open for 1% -> 1% of each run, Pallas kernels for 0% -> 0%
where the time goes in v8:
time: 201 us; the launch traced here: 200 us
  blocking collectives  82.4 us (41%)
  waiting for transfers between devices  62.2 us (31%)
  starting transfers between devices  25.1 us (12%)
  matrix products  13.1 us (7%)
  local copies, waits for them, and re-layouts  11 us (5%)
  other arithmetic  5.6 us (3%)
    ppermute x1, waiting for transfers between devices, layer(): partner_part = lax.ppermute(sent_half, 'pipe', mirror)  56.3 us
    all_to_all x1, blocking collectives, layer(): arrived = lax.all_to_all(payload, 'eg', 0, 0, tiled=True)  44.6 us
    all_to_all x1, blocking collectives, layer(): across = lax.all_to_all(on_chip, 'xs', 0, 0, tiled=True)  19.5 us
    all_to_all x1, blocking collectives, layer(): pair = lax.all_to_all(pair, 'xs', 0, 0, tiled=True)  18.3 us
    ppermute x1, starting transfers between devices, layer(): partner_part = lax.ppermute(sent_half, 'pipe', mirror)  10.7 us
    all_to_all x1, starting transfers between devices, layer(): returned = lax.all_to_all(summed, 'eg', 0, 0, tiled=True)  10.4 us
    reshape x1, local copies, waits for them, and re-layouts, layer(): gathered.reshape(shards * experts_here * capacity, 2 * model_width)  4.03 us
  transfers between devices with their start and end apart: 4, of which 3 were waited for; matrix products, arithmetic and copies ran while one was open for 1% of the time, Pallas kernels for 0%

profile of v8, /device:TPU:128, one launch (start us, length us, event | category | flops | bytes accessed | tf_op | source)
XLA Modules:
  0.0 200.3 jit_solution(13338891518195412061)
XLA Ops:
  0.7 0.8 fusion.25
  2.8 1.3 convolution_convert_fusion.4
  4.1 1.1 multiply_convert_fusion
  5.2 0.8 reshape.45
  6.0 44.6 %all_to_all.20 = bf16[16,16,1280]{2,1,0:T(8,128)(2,1)S(1)} all-to-all(bf16[16,16,1280]{2,1,0:T(8,128)(2,1)S(1)} %reshape.45), channel_id=1, replica_groups=mesh['pipe'=8,'eg'=16,'xs'=2,'core'=2] {'eg'}, dimensions={0} | all-to-all | bytes 1310720 | tf_op jit(solution)/shard_map/all_to_all | solution.py:70
  50.7 18.3 %all_to_all.21 = bf16[32,16,1280]{2,1,0:T(8,128)(2,1)S(1)} all-to-all(bf16[32,16,1280]{2,1,0:T(8,128)(2,1)S(1)} %bitcast.33), channel_id=1, replica_groups=mesh['pipe'=8,'eg'=16,'xs'=2,'core'=2] {'xs'}, dimensions={0} | all-to-all | bytes 2621440 | tf_op jit(solution)/shard_map/all_to_all | solution.py:74
  69.0 1.9 collective-permute-start
  71.0 3.0 %collective-permute-done = bf16[32,16,1280]{2,1,0:T(8,128)(2,1)S(1)} collective-permute-done((bf16[32,16,1280]{2,1,0:T(8,128)(2,1)S(1)}, bf16[32,16,1280]{2,1,0:T(8,128)(2,1)S(1)}, u32[]{:S(2)}, u32[]{:S(2)}) %collective-permute-start) | collective-permute-done | bytes 1310752 | tf_op jit(solution)/shard_map/ppermute | solution.py:76
  74.2 4.0 %reshape.47 = bf16[320,4096]{1,0:T(8,128)(2,1)} reshape(bf16[64,16,1280]{2,1,0:T(8,128)(2,1)S(1)} %pad_maximum_fusion) | data formatting | bytes 5242880 | tf_op jit(solution)/shard_map/reshape | solution.py:77
  78.2 2.3 %fusion.7 = f32[320,192]{0,1:T(8,128)S(1)} fusion(bf16[320,4096]{1,0:T(8,128)(2,1)} %reshape.47, bf16[1,2048,192]{1,2,0:T(8,128)(2,1)} %param.11), kind=kOutput, calls=%fused_computation.18 | convolution fusion | flops 251658240 | bytes 2342912 | tf_op jit(solution)/shard_map/dot_general | solution.py:17
  80.6 1.8 fusion.3
  85.9 2.0 %collective-permute-start.1 = (bf16[160,4096]{1,0:T(8,128)(2,1)S(1)}, bf16[160,4096]{1,0:T(8,128)(2,1)S(1)}, u32[]{:S(2)}, u32[]{:S(2)}) collective-permute-start(bf16[160,4096]{1,0:T(8,128)(2,1)S(1)} %pad_maximum_fusion.1), channel_id=1, source_target_pairs={{0,1},{1,0},{2,3},{3,2},{4,5},{5,4},{6,7},{7,6},{8,9},{9,8},{10,11... | collective-permute-start | bytes 3932168 | tf_op jit(solution)/shard_map/ppermute | solution.py:85
  88.0 2.9 %collective-permute-done.1 = bf16[160,4096]{1,0:T(8,128)(2,1)S(1)} collective-permute-done((bf16[160,4096]{1,0:T(8,128)(2,1)S(1)}, bf16[160,4096]{1,0:T(8,128)(2,1)S(1)}, u32[]{:S(2)}, u32[]{:S(2)}) %collective-permute-start.1) | collective-permute-done | bytes 1310752 | tf_op jit(solution)/shard_map/ppermute | solution.py:85
  91.3 19.5 %all_to_all.22 = bf16[2,80,4096]{2,1,0:T(8,128)(2,1)S(1)} all-to-all(bf16[2,80,4096]{2,1,0:T(8,128)(2,1)S(1)} %bitcast.32), channel_id=1, replica_groups=mesh['pipe'=8,'eg'=16,'xs'=2,'core'=2] {'xs'}, dimensions={0} | all-to-all | bytes 2621440 | tf_op jit(solution)/shard_map/all_to_all | solution.py:88
  110.7 1.2 reduce_sum.59
  112.0 2.8 %reshape.49 = bf16[16,16,1280]{2,1,0:T(8,128)(2,1)} reshape(bf16[80,4096]{1,0:T(8,128)(2,1)} %reduce_sum.59) | data formatting | bytes 1310720 | tf_op jit(solution)/shard_map/reshape | solution.py:90
  114.8 10.4 %all-to-all-start.3 = ((bf16[16,16,1280]{2,1,0:T(8,128)(2,1)}), bf16[16,16,1280]{2,1,0:T(8,128)(2,1)}, u32[]{:S(2)}, u32[]{:S(2)}) async-start(bf16[16,16,1280]{2,1,0:T(8,128)(2,1)} %reshape.49), calls=%async_computation.3 | async-start | bytes 1310720 | tf_op jit(solution)/shard_map/all_to_all | solution.py:91
  125.3 1.5 convolution_convert_fusion.1
  126.8 10.7 %collective-permute-start.2 = (bf16[192,1024]{1,0:T(8,128)(2,1)S(1)}, bf16[192,1024]{1,0:T(8,128)(2,1)S(1)}, u32[]{:S(2)}, u32[]{:S(2)}) collective-permute-start(bf16[192,1024]{1,0:T(8,128)(2,1)S(1)} %broadcast_select_fusion), channel_id=1, source_target_pairs={{0,448},{64,384},{128,320},{192,256},{256,192},{320,128},{384,64},... | collective-permute-start | bytes 1179656 | tf_op jit(solution)/shard_map/ppermute | solution.py:114
  137.5 56.3 %collective-permute-done.2 = bf16[192,1024]{1,0:T(8,128)(2,1)S(1)} collective-permute-done((bf16[192,1024]{1,0:T(8,128)(2,1)S(1)}, bf16[192,1024]{1,0:T(8,128)(2,1)S(1)}, u32[]{:S(2)}, u32[]{:S(2)}) %collective-permute-start.2) | collective-permute-done | bytes 393248 | tf_op jit(solution)/shard_map/ppermute | solution.py:114
  193.8 0.9 fusion.17
  194.8 1.9 reshape.50
  196.7 1.1 convolution_convert_fusion.2
  197.8 1.4 convolution_convert_fusion.3
  (45 shorter events, 6.5 us)
Async XLA Ops:
  0.6 81.8 %copy-start = (bf16[1,2048,192]{1,2,0:T(8,128)(2,1)S(1)}, bf16[1,2048,192]{1,2,0:T(8,128)(2,1)}, u32[]{:S(2)}) copy-start(bf16[1,2048,192]{1,2,0:T(8,128)(2,1)} %param.12) | copy-start | bytes 2359300
  0.6 3.4 %copy-start.6 = (bf16[128,2048]{1,0:T(8,128)(2,1)S(1)}, bf16[128,2048]{1,0:T(8,128)(2,1)}, u32[]{:S(2)}) copy-start(bf16[128,2048]{1,0:T(8,128)(2,1)} %param.8) | copy-start | bytes 1572868
  69.0 4.9 %collective-permute-start = (bf16[32,16,1280]{2,1,0:T(8,128)(2,1)S(1)}, bf16[32,16,1280]{2,1,0:T(8,128)(2,1)S(1)}, u32[]{:S(2)}, u32[]{:S(2)}) collective-permute-start(bf16[32,16,1280]{2,1,0:T(8,128)(2,1)S(1)} %all_to_all.21), channel_id=1, source_target_pairs={{0,1},{1,0},{2,3},{3,2},{4,5},{5,4},{6,7},{7,6},{8,9},{9,8},{10,11... | collective-permute-start | bytes 3932168 | tf_op jit(solution)/shard_map/ppermute | solution.py:76
  78.2 2.4 %copy-start.1 = (bf16[320,4096]{1,0:T(8,128)(2,1)S(1)}, bf16[320,4096]{1,0:T(8,128)(2,1)}, u32[]{:S(2)}) copy-start(bf16[320,4096]{1,0:T(8,128)(2,1)} %reshape.47) | copy-start | bytes 7864324
  82.4 1.1 copy-start.4
  83.1 1.6 copy-start.7
  84.1 1.1 copy-start.5
  85.9 4.9 %collective-permute-start.1 = (bf16[160,4096]{1,0:T(8,128)(2,1)S(1)}, bf16[160,4096]{1,0:T(8,128)(2,1)S(1)}, u32[]{:S(2)}, u32[]{:S(2)}) collective-permute-start(bf16[160,4096]{1,0:T(8,128)(2,1)S(1)} %pad_maximum_fusion.1), channel_id=1, source_target_pairs={{0,1},{1,0},{2,3},{3,2},{4,5},{5,4},{6,7},{7,6},{8,9},{9,8},{10,11... | collective-permute-start | bytes 3932168 | tf_op jit(solution)/shard_map/ppermute | solution.py:85
  112.0 13.3 %copy-start.2 = (bf16[320,4096]{1,0:T(8,128)(2,1)S(1)}, bf16[320,4096]{1,0:T(8,128)(2,1)}, u32[]{:S(2)}) copy-start(bf16[320,4096]{1,0:T(8,128)(2,1)} %reshape.47) | copy-start | bytes 7864324
  114.8 80.0 %all-to-all-start.3 = ((bf16[16,16,1280]{2,1,0:T(8,128)(2,1)}), bf16[16,16,1280]{2,1,0:T(8,128)(2,1)}, u32[]{:S(2)}, u32[]{:S(2)}) async-start(bf16[16,16,1280]{2,1,0:T(8,128)(2,1)} %reshape.49), calls=%async_computation.3 | async-start | bytes 1310720 | tf_op jit(solution)/shard_map/all_to_all | solution.py:91
  126.8 67.0 %collective-permute-start.2 = (bf16[192,1024]{1,0:T(8,128)(2,1)S(1)}, bf16[192,1024]{1,0:T(8,128)(2,1)S(1)}, u32[]{:S(2)}, u32[]{:S(2)}) collective-permute-start(bf16[192,1024]{1,0:T(8,128)(2,1)S(1)} %broadcast_select_fusion), channel_id=1, source_target_pairs={{0,448},{64,384},{128,320},{192,256},{256,192},{320,128},{384,64},... | collective-permute-start | bytes 1179656 | tf_op jit(solution)/shard_map/ppermute | solution.py:114
  194.8 4.5 %copy-start.3 = (f32[80,2048]{1,0:T(8,128)S(1)}, f32[80,2048]{1,0:T(8,128)}, u32[]{:S(2)}) copy-start(f32[80,2048]{1,0:T(8,128)} %get-tuple-element.5) | copy-start | bytes 1966084
  196.7 2.9 %copy-start.8 = (s32[128,8]{0,1:T(8,128)S(1)}, s32[128,8]{0,1:T(8,128)}, u32[]{:S(2)}) copy-start(s32[128,8]{0,1:T(8,128)} %param.9) | copy-start | bytes 12292

commit v9 on v8

--- a/solution.py
+++ b/solution.py
@@ -68,11 +68,8 @@
         experts_here, tile_rows, -1
     )
     arrived = lax.all_to_all(payload, "eg", 0, 0, tiled=True)
-    pair = jnp.broadcast_to(arrived[None], (2,) + arrived.shape).reshape(
-        (2 * experts_here,) + arrived.shape[1:]
-    )
-    pair = lax.all_to_all(pair, "xs", 0, 0, tiled=True)
     swap = [(0, 1), (1, 0)]
+    pair = jnp.concatenate([arrived, lax.ppermute(arrived, "xs", swap)])
     gathered = jnp.concatenate([pair, lax.ppermute(pair, "core", swap)])
     gathered = gathered.reshape(shards * experts_here * capacity, 2 * model_width)
     inputs = gathered[:, :model_width]
@@ -85,8 +82,8 @@
     other = lax.ppermute(parts[1], "core", swap)
     on_chip = (parts[0].astype(jnp.float32) + other.astype(jnp.float32)).astype(jnp.bfloat16)
     on_chip = on_chip.reshape(2, slot_count, -1)
-    across = lax.all_to_all(on_chip, "xs", 0, 0, tiled=True)
-    summed = across.astype(jnp.float32).sum(axis=0)
+    across = lax.ppermute(on_chip[1], "xs", swap)
+    summed = on_chip[0].astype(jnp.float32) + across.astype(jnp.float32)
     summed = summed.astype(jnp.bfloat16).reshape(experts_here, tile_rows, -1)
     returned = lax.all_to_all(summed, "eg", 0, 0, tiled=True)
     returned = returned.reshape(slot_count, 2 * model_width).astype(jnp.float32)

time: 201 us -> 199 us (0.990)
  blocking collectives: 82.4 us -> 44.6 us
  waiting for transfers between devices: 62.2 us -> 93.5 us
  starting transfers between devices: 25.1 us -> 30 us
    all_to_all x2 -> x0, blocking collectives: 37.8 us -> none  [the longest x1 19.5 us: layer(): across = lax.all_to_all(on_chip, 'xs', 0, 0, tiled=True)]
    ppermute x0 -> x2, waiting for transfers between devices: none -> 31.2 us  [the longest x1 16.2 us: layer(): across = lax.ppermute(on_chip[1], 'xs', swap)]
    ppermute x0 -> x2, starting transfers between devices: none -> 4.97 us  [the longest x1 2.49 us: layer(): across = lax.ppermute(on_chip[1], 'xs', swap)]
  transfers between devices with their start and end apart: 4 -> 6, of which waited for: 3 -> 5; matrix products, arithmetic and copies ran while one was open for 1% -> 1% of each run, Pallas kernels for 0% -> 0%
where the time goes in v9:
time: 199 us; the launch traced here: 198 us
  waiting for transfers between devices  93.5 us (47%)
  blocking collectives  44.6 us (22%)
  starting transfers between devices  30 us (15%)
  matrix products  13.1 us (7%)
  local copies, waits for them, and re-layouts  10.7 us (5%)
  other arithmetic  5.51 us (3%)
    ppermute x1, waiting for transfers between devices, layer(): partner_part = lax.ppermute(sent_half, 'pipe', mirror)  56.4 us
    all_to_all x1, blocking collectives, layer(): arrived = lax.all_to_all(payload, 'eg', 0, 0, tiled=True)  44.6 us
    ppermute x1, waiting for transfers between devices, layer(): across = lax.ppermute(on_chip[1], 'xs', swap)  16.2 us
    ppermute x1, waiting for transfers between devices, layer(): pair = jnp.concatenate([arrived, lax.ppermute(arrived, 'xs', swap)])  15.1 us
    ppermute x1, starting transfers between devices, layer(): partner_part = lax.ppermute(sent_half, 'pipe', mirror)  10.7 us
    all_to_all x1, starting transfers between devices, layer(): returned = lax.all_to_all(summed, 'eg', 0, 0, tiled=True)  10.4 us
    reshape x1, local copies, waits for them, and re-layouts, layer(): gathered.reshape(shards * experts_here * capacity, 2 * model_width)  4.03 us
  transfers between devices with their start and end apart: 6, of which 5 were waited for; matrix products, arithmetic and copies ran while one was open for 1% of the time, Pallas kernels for 0%

profile of v9, /device:TPU:128, one launch (start us, length us, event | category | flops | bytes accessed | tf_op | source)
XLA Modules:
  0.0 198.4 jit_solution(7306488067164580938)
XLA Ops:
  2.8 1.3 convolution_convert_fusion.4
  4.1 1.1 multiply_convert_fusion
  6.0 44.6 %all_to_all.10 = bf16[16,16,1280]{2,1,0:T(8,128)(2,1)S(1)} all-to-all(bf16[16,16,1280]{2,1,0:T(8,128)(2,1)S(1)} %reshape.43), channel_id=1, replica_groups=mesh['pipe'=8,'eg'=16,'xs'=2,'core'=2] {'eg'}, dimensions={0} | all-to-all | bytes 1310720 | tf_op jit(solution)/shard_map/all_to_all | solution.py:70
  50.6 2.5 %collective-permute-start = (bf16[16,16,1280]{2,1,0:T(8,128)(2,1)S(1)}, bf16[16,16,1280]{2,1,0:T(8,128)(2,1)S(1)}, u32[]{:S(2)}, u32[]{:S(2)}) collective-permute-start(bf16[16,16,1280]{2,1,0:T(8,128)(2,1)S(1)} %all_to_all.10), channel_id=1, source_target_pairs={{0,2},{2,0},{1,3},{3,1},{4,6},{6,4},{5,7},{7,5},{8,10},{10,8},{9,1... | collective-permute-start | bytes 1966088 | tf_op jit(solution)/shard_map/ppermute | solution.py:72
  53.1 15.1 %collective-permute-done = bf16[16,16,1280]{2,1,0:T(8,128)(2,1)S(1)} collective-permute-done((bf16[16,16,1280]{2,1,0:T(8,128)(2,1)S(1)}, bf16[16,16,1280]{2,1,0:T(8,128)(2,1)S(1)}, u32[]{:S(2)}, u32[]{:S(2)}) %collective-permute-start) | collective-permute-done | bytes 655392 | tf_op jit(solution)/shard_map/ppermute | solution.py:72
  68.3 1.9 collective-permute-start.1
  70.2 3.0 %collective-permute-done.1 = bf16[32,16,1280]{2,1,0:T(8,128)(2,1)S(1)} collective-permute-done((bf16[32,16,1280]{2,1,0:T(8,128)(2,1)S(1)}, bf16[32,16,1280]{2,1,0:T(8,128)(2,1)S(1)}, u32[]{:S(2)}, u32[]{:S(2)}) %collective-permute-start.1) | collective-permute-done | bytes 1310752 | tf_op jit(solution)/shard_map/ppermute | solution.py:73
  73.4 4.0 %reshape.44 = bf16[320,4096]{1,0:T(8,128)(2,1)} reshape(bf16[64,16,1280]{2,1,0:T(8,128)(2,1)S(1)} %pad_maximum_fusion) | data formatting | bytes 5242880 | tf_op jit(solution)/shard_map/reshape | solution.py:74
  77.5 2.3 %fusion.7 = f32[320,192]{0,1:T(8,128)S(1)} fusion(bf16[320,4096]{1,0:T(8,128)(2,1)} %reshape.44, bf16[1,2048,192]{1,2,0:T(8,128)(2,1)} %param.11), kind=kOutput, calls=%fused_computation.20 | convolution fusion | flops 251658240 | bytes 2342912 | tf_op jit(solution)/shard_map/dot_general | solution.py:17
  79.8 1.8 fusion.3
  85.2 2.0 %collective-permute-start.2 = (bf16[160,4096]{1,0:T(8,128)(2,1)S(1)}, bf16[160,4096]{1,0:T(8,128)(2,1)S(1)}, u32[]{:S(2)}, u32[]{:S(2)}) collective-permute-start(bf16[160,4096]{1,0:T(8,128)(2,1)S(1)} %pad_maximum_fusion.1), channel_id=1, source_target_pairs={{0,1},{1,0},{2,3},{3,2},{4,5},{5,4},{6,7},{7,6},{8,9},{9,8},{10,11... | collective-permute-start | bytes 3932168 | tf_op jit(solution)/shard_map/ppermute | solution.py:82
  87.2 2.9 %collective-permute-done.2 = bf16[160,4096]{1,0:T(8,128)(2,1)S(1)} collective-permute-done((bf16[160,4096]{1,0:T(8,128)(2,1)S(1)}, bf16[160,4096]{1,0:T(8,128)(2,1)S(1)}, u32[]{:S(2)}, u32[]{:S(2)}) %collective-permute-start.2) | collective-permute-done | bytes 1310752 | tf_op jit(solution)/shard_map/ppermute | solution.py:82
  90.6 2.5 %collective-permute-start.3 = (bf16[80,4096]{1,0:T(8,128)(2,1)S(1)}, bf16[80,4096]{1,0:T(8,128)(2,1)S(1)}, u32[]{:S(2)}, u32[]{:S(2)}) collective-permute-start(bf16[80,4096]{1,0:T(8,128)(2,1)S(1)} %slice.53), channel_id=1, source_target_pairs={{0,2},{2,0},{1,3},{3,1},{4,6},{6,4},{5,7},{7,5},{8,10},{10,8},{9,1... | collective-permute-start | bytes 1966088 | tf_op jit(solution)/shard_map/ppermute | solution.py:85
  93.1 16.2 %collective-permute-done.3 = bf16[80,4096]{1,0:T(8,128)(2,1)S(1)} collective-permute-done((bf16[80,4096]{1,0:T(8,128)(2,1)S(1)}, bf16[80,4096]{1,0:T(8,128)(2,1)S(1)}, u32[]{:S(2)}, u32[]{:S(2)}) %collective-permute-start.3) | collective-permute-done | bytes 655392 | tf_op jit(solution)/shard_map/ppermute | solution.py:85
  109.2 1.0 add_convert_fusion.1
  110.2 2.7 %reshape.45 = bf16[16,16,1280]{2,1,0:T(8,128)(2,1)} reshape(bf16[80,4096]{1,0:T(8,128)(2,1)} %add_convert_fusion.1) | data formatting | bytes 1310720 | tf_op jit(solution)/shard_map/reshape | solution.py:87
  112.9 10.4 %all-to-all-start.1 = ((bf16[16,16,1280]{2,1,0:T(8,128)(2,1)}), bf16[16,16,1280]{2,1,0:T(8,128)(2,1)}, u32[]{:S(2)}, u32[]{:S(2)}) async-start(bf16[16,16,1280]{2,1,0:T(8,128)(2,1)} %reshape.45), calls=%async_computation.1 | async-start | bytes 1310720 | tf_op jit(solution)/shard_map/all_to_all | solution.py:88
  123.4 1.5 convolution_convert_fusion.1
  124.9 10.7 %collective-permute-start.4 = (bf16[192,1024]{1,0:T(8,128)(2,1)S(1)}, bf16[192,1024]{1,0:T(8,128)(2,1)S(1)}, u32[]{:S(2)}, u32[]{:S(2)}) collective-permute-start(bf16[192,1024]{1,0:T(8,128)(2,1)S(1)} %broadcast_select_fusion), channel_id=1, source_target_pairs={{0,448},{64,384},{128,320},{192,256},{256,192},{320,128},{384,64},... | collective-permute-start | bytes 1179656 | tf_op jit(solution)/shard_map/ppermute | solution.py:111
  135.6 56.4 %collective-permute-done.4 = bf16[192,1024]{1,0:T(8,128)(2,1)S(1)} collective-permute-done((bf16[192,1024]{1,0:T(8,128)(2,1)S(1)}, bf16[192,1024]{1,0:T(8,128)(2,1)S(1)}, u32[]{:S(2)}, u32[]{:S(2)}) %collective-permute-start.4) | collective-permute-done | bytes 393248 | tf_op jit(solution)/shard_map/ppermute | solution.py:111
  191.9 0.9 fusion.17
  192.9 1.9 reshape.46
  194.8 1.1 convolution_convert_fusion.2
  195.9 1.4 convolution_convert_fusion.3
  (46 shorter events, 8.2 us)
Async XLA Ops:
  0.6 81.0 %copy-start = (bf16[1,2048,192]{1,2,0:T(8,128)(2,1)S(1)}, bf16[1,2048,192]{1,2,0:T(8,128)(2,1)}, u32[]{:S(2)}) copy-start(bf16[1,2048,192]{1,2,0:T(8,128)(2,1)} %param.12) | copy-start | bytes 2359300
  0.6 3.4 %copy-start.5 = (bf16[128,2048]{1,0:T(8,128)(2,1)S(1)}, bf16[128,2048]{1,0:T(8,128)(2,1)}, u32[]{:S(2)}) copy-start(bf16[128,2048]{1,0:T(8,128)(2,1)} %param.8) | copy-start | bytes 1572868
  50.6 17.5 %collective-permute-start = (bf16[16,16,1280]{2,1,0:T(8,128)(2,1)S(1)}, bf16[16,16,1280]{2,1,0:T(8,128)(2,1)S(1)}, u32[]{:S(2)}, u32[]{:S(2)}) collective-permute-start(bf16[16,16,1280]{2,1,0:T(8,128)(2,1)S(1)} %all_to_all.10), channel_id=1, source_target_pairs={{0,2},{2,0},{1,3},{3,1},{4,6},{6,4},{5,7},{7,5},{8,10},{10,8},{9,1... | collective-permute-start | bytes 1966088 | tf_op jit(solution)/shard_map/ppermute | solution.py:72
  68.3 4.9 %collective-permute-start.1 = (bf16[32,16,1280]{2,1,0:T(8,128)(2,1)S(1)}, bf16[32,16,1280]{2,1,0:T(8,128)(2,1)S(1)}, u32[]{:S(2)}, u32[]{:S(2)}) collective-permute-start(bf16[32,16,1280]{2,1,0:T(8,128)(2,1)S(1)} %pad_maximum_fusion.2), channel_id=1, source_target_pairs={{0,1},{1,0},{2,3},{3,2},{4,5},{5,4},{6,7},{7,6},{8,9},{9,8},{10,11... | collective-permute-start | bytes 3932168 | tf_op jit(solution)/shard_map/ppermute | solution.py:73
  77.5 2.4 %copy-start.1 = (bf16[320,4096]{1,0:T(8,128)(2,1)S(1)}, bf16[320,4096]{1,0:T(8,128)(2,1)}, u32[]{:S(2)}) copy-start(bf16[320,4096]{1,0:T(8,128)(2,1)} %reshape.44) | copy-start | bytes 7864324
  81.7 1.1 copy-start.3
  82.4 1.6 copy-start.6
  83.4 1.1 copy-start.4
  85.2 4.9 %collective-permute-start.2 = (bf16[160,4096]{1,0:T(8,128)(2,1)S(1)}, bf16[160,4096]{1,0:T(8,128)(2,1)S(1)}, u32[]{:S(2)}, u32[]{:S(2)}) collective-permute-start(bf16[160,4096]{1,0:T(8,128)(2,1)S(1)} %pad_maximum_fusion.1), channel_id=1, source_target_pairs={{0,1},{1,0},{2,3},{3,2},{4,5},{5,4},{6,7},{7,6},{8,9},{9,8},{10,11... | collective-permute-start | bytes 3932168 | tf_op jit(solution)/shard_map/ppermute | solution.py:82
  90.6 18.7 %collective-permute-start.3 = (bf16[80,4096]{1,0:T(8,128)(2,1)S(1)}, bf16[80,4096]{1,0:T(8,128)(2,1)S(1)}, u32[]{:S(2)}, u32[]{:S(2)}) collective-permute-start(bf16[80,4096]{1,0:T(8,128)(2,1)S(1)} %slice.53), channel_id=1, source_target_pairs={{0,2},{2,0},{1,3},{3,1},{4,6},{6,4},{5,7},{7,5},{8,10},{10,8},{9,1... | collective-permute-start | bytes 1966088 | tf_op jit(solution)/shard_map/ppermute | solution.py:85
  112.9 80.0 %all-to-all-start.1 = ((bf16[16,16,1280]{2,1,0:T(8,128)(2,1)}), bf16[16,16,1280]{2,1,0:T(8,128)(2,1)}, u32[]{:S(2)}, u32[]{:S(2)}) async-start(bf16[16,16,1280]{2,1,0:T(8,128)(2,1)} %reshape.45), calls=%async_computation.1 | async-start | bytes 1310720 | tf_op jit(solution)/shard_map/all_to_all | solution.py:88
  124.9 67.0 %collective-permute-start.4 = (bf16[192,1024]{1,0:T(8,128)(2,1)S(1)}, bf16[192,1024]{1,0:T(8,128)(2,1)S(1)}, u32[]{:S(2)}, u32[]{:S(2)}) collective-permute-start(bf16[192,1024]{1,0:T(8,128)(2,1)S(1)} %broadcast_select_fusion), channel_id=1, source_target_pairs={{0,448},{64,384},{128,320},{192,256},{256,192},{320,128},{384,64},... | collective-permute-start | bytes 1179656 | tf_op jit(solution)/shard_map/ppermute | solution.py:111
  192.9 4.5 %copy-start.2 = (f32[80,2048]{1,0:T(8,128)S(1)}, f32[80,2048]{1,0:T(8,128)}, u32[]{:S(2)}) copy-start(f32[80,2048]{1,0:T(8,128)} %get-tuple-element.5) | copy-start | bytes 1966084
  194.8 2.9 %copy-start.7 = (s32[128,8]{0,1:T(8,128)S(1)}, s32[128,8]{0,1:T(8,128)}, u32[]{:S(2)}) copy-start(s32[128,8]{0,1:T(8,128)} %param.9) | copy-start | bytes 12292

commit v10 on v9

--- a/solution.py
+++ b/solution.py
@@ -69,8 +69,9 @@
     )
     arrived = lax.all_to_all(payload, "eg", 0, 0, tiled=True)
     swap = [(0, 1), (1, 0)]
-    pair = jnp.concatenate([arrived, lax.ppermute(arrived, "xs", swap)])
-    gathered = jnp.concatenate([pair, lax.ppermute(pair, "core", swap)])
+    partner = lax.ppermute(arrived, "xs", swap)
+    beside = lax.ppermute(arrived, "core", swap)
+    gathered = jnp.concatenate([arrived, partner, beside, lax.ppermute(partner, "core", swap)])
     gathered = gathered.reshape(shards * experts_here * capacity, 2 * model_width)
     inputs = gathered[:, :model_width]
     scaled = gathered[:, model_width:]

time: 199 us -> 199 us (level)
  waiting for transfers between devices: 93.5 us -> 90.4 us
  starting transfers between devices: 30 us -> 32.1 us
    ppermute x2 -> x3, waiting for transfers between devices: 18.1 us -> 15.2 us  [the longest x1 13.1 us: layer(): partner = lax.ppermute(arrived, 'xs', swap)]
    ppermute x2 -> x3, starting transfers between devices: 4.4 us -> 6.32 us  [the longest x1 2.49 us: layer(): partner = lax.ppermute(arrived, 'xs', swap)]
  transfers between devices with their start and end apart: 6 -> 7, of which waited for: 5 -> 5; matrix products, arithmetic and copies ran while one was open for 1% -> 1% of each run, Pallas kernels for 0% -> 0%
where the time goes in v10:
time: 199 us; the launch traced here: 198 us
  waiting for transfers between devices  90.4 us (45%)
  blocking collectives  44.6 us (22%)
  starting transfers between devices  32.1 us (16%)
  matrix products  14.1 us (7%)
  local copies, waits for them, and re-layouts  10.7 us (5%)
  other arithmetic  5.47 us (3%)
    ppermute x1, waiting for transfers between devices, layer(): partner_part = lax.ppermute(sent_half, 'pipe', mirror)  56.2 us
    all_to_all x1, blocking collectives, layer(): arrived = lax.all_to_all(payload, 'eg', 0, 0, tiled=True)  44.6 us
    ppermute x1, waiting for transfers between devices, layer(): across = lax.ppermute(on_chip[1], 'xs', swap)  16.2 us
    ppermute x1, waiting for transfers between devices, layer(): partner = lax.ppermute(arrived, 'xs', swap)  13.1 us
    ppermute x1, starting transfers between devices, layer(): partner_part = lax.ppermute(sent_half, 'pipe', mirror)  10.8 us
    all_to_all x1, starting transfers between devices, layer(): returned = lax.all_to_all(summed, 'eg', 0, 0, tiled=True)  10.5 us
    reshape x1, local copies, waits for them, and re-layouts, layer(): gathered.reshape(shards * experts_here * capacity, 2 * model_width)  4.03 us
  transfers between devices with their start and end apart: 7, of which 5 were waited for; matrix products, arithmetic and copies ran while one was open for 1% of the time, Pallas kernels for 0%

profile of v10, /device:TPU:128, one launch (start us, length us, event | category | flops | bytes accessed | tf_op | source)
XLA Modules:
  0.0 198.3 jit_solution(4326239921546067334)
XLA Ops:
  2.7 1.3 convolution_convert_fusion.4
  4.0 2.1 %multiply_convert_fusion = (bf16[80,2048]{1,0:T(8,128)(2,1)S(1)}, f32[80,2048]{1,0:T(8,128)}) fusion(f32[80]{0:T(128)S(1)} %mul.76, bf16[128,2048]{1,0:T(8,128)(2,1)} %param.8, f32[80,128]{1,0:T(8,128)S(1)} %compare_select_fusion), kind=kOutput, calls=%fused_computation.33 | convolution fusion | flops 42280960 | bytes 1548608 | tf_op jit(solution)/shard_map/dot_general | solution.py:63
  7.0 44.6 %all_to_all.10 = bf16[16,16,1280]{2,1,0:T(8,128)(2,1)S(1)} all-to-all(bf16[16,16,1280]{2,1,0:T(8,128)(2,1)S(1)} %reshape.43), channel_id=1, replica_groups=mesh['pipe'=8,'eg'=16,'xs'=2,'core'=2] {'eg'}, dimensions={0} | all-to-all | bytes 1310720 | tf_op jit(solution)/shard_map/all_to_all | solution.py:70
  51.6 2.5 %collective-permute-start = (bf16[16,16,1280]{2,1,0:T(8,128)(2,1)S(1)}, bf16[16,16,1280]{2,1,0:T(8,128)(2,1)S(1)}, u32[]{:S(2)}, u32[]{:S(2)}) collective-permute-start(bf16[16,16,1280]{2,1,0:T(8,128)(2,1)S(1)} %all_to_all.10), channel_id=1, source_target_pairs={{0,2},{2,0},{1,3},{3,1},{4,6},{6,4},{5,7},{7,5},{8,10},{10,8},{9,1... | collective-permute-start | bytes 1966088 | tf_op jit(solution)/shard_map/ppermute | solution.py:72
  54.1 1.9 collective-permute-start.1
  56.0 13.1 %collective-permute-done = bf16[16,16,1280]{2,1,0:T(8,128)(2,1)S(1)} collective-permute-done((bf16[16,16,1280]{2,1,0:T(8,128)(2,1)S(1)}, bf16[16,16,1280]{2,1,0:T(8,128)(2,1)S(1)}, u32[]{:S(2)}, u32[]{:S(2)}) %collective-permute-start) | collective-permute-done | bytes 655392 | tf_op jit(solution)/shard_map/ppermute | solution.py:72
  69.1 1.9 collective-permute-start.2
  71.0 2.1 %collective-permute-done.2 = bf16[16,16,1280]{2,1,0:T(8,128)(2,1)S(1)} collective-permute-done((bf16[16,16,1280]{2,1,0:T(8,128)(2,1)S(1)}, bf16[16,16,1280]{2,1,0:T(8,128)(2,1)S(1)}, u32[]{:S(2)}, u32[]{:S(2)}) %collective-permute-start.2) | collective-permute-done | bytes 655392 | tf_op jit(solution)/shard_map/ppermute | solution.py:74
  73.5 4.0 %reshape.44 = bf16[320,4096]{1,0:T(8,128)(2,1)} reshape(bf16[64,16,1280]{2,1,0:T(8,128)(2,1)S(1)} %pad_maximum_fusion) | data formatting | bytes 5242880 | tf_op jit(solution)/shard_map/reshape | solution.py:75
  77.5 2.3 %fusion.7 = f32[320,192]{0,1:T(8,128)S(1)} fusion(bf16[320,4096]{1,0:T(8,128)(2,1)} %reshape.44, bf16[1,2048,192]{1,2,0:T(8,128)(2,1)} %param.11), kind=kOutput, calls=%fused_computation.19 | convolution fusion | flops 251658240 | bytes 2342912 | tf_op jit(solution)/shard_map/dot_general | solution.py:17
  79.9 1.8 fusion.3
  85.2 2.0 %collective-permute-start.3 = (bf16[160,4096]{1,0:T(8,128)(2,1)S(1)}, bf16[160,4096]{1,0:T(8,128)(2,1)S(1)}, u32[]{:S(2)}, u32[]{:S(2)}) collective-permute-start(bf16[160,4096]{1,0:T(8,128)(2,1)S(1)} %pad_maximum_fusion.1), channel_id=1, source_target_pairs={{0,1},{1,0},{2,3},{3,2},{4,5},{5,4},{6,7},{7,6},{8,9},{9,8},{10,11... | collective-permute-start | bytes 3932168 | tf_op jit(solution)/shard_map/ppermute | solution.py:83
  87.2 2.9 %collective-permute-done.3 = bf16[160,4096]{1,0:T(8,128)(2,1)S(1)} collective-permute-done((bf16[160,4096]{1,0:T(8,128)(2,1)S(1)}, bf16[160,4096]{1,0:T(8,128)(2,1)S(1)}, u32[]{:S(2)}, u32[]{:S(2)}) %collective-permute-start.3) | collective-permute-done | bytes 1310752 | tf_op jit(solution)/shard_map/ppermute | solution.py:83
  90.6 2.5 %collective-permute-start.4 = (bf16[80,4096]{1,0:T(8,128)(2,1)S(1)}, bf16[80,4096]{1,0:T(8,128)(2,1)S(1)}, u32[]{:S(2)}, u32[]{:S(2)}) collective-permute-start(bf16[80,4096]{1,0:T(8,128)(2,1)S(1)} %slice.53), channel_id=1, source_target_pairs={{0,2},{2,0},{1,3},{3,1},{4,6},{6,4},{5,7},{7,5},{8,10},{10,8},{9,1... | collective-permute-start | bytes 1966088 | tf_op jit(solution)/shard_map/ppermute | solution.py:86
  93.1 16.2 %collective-permute-done.4 = bf16[80,4096]{1,0:T(8,128)(2,1)S(1)} collective-permute-done((bf16[80,4096]{1,0:T(8,128)(2,1)S(1)}, bf16[80,4096]{1,0:T(8,128)(2,1)S(1)}, u32[]{:S(2)}, u32[]{:S(2)}) %collective-permute-start.4) | collective-permute-done | bytes 655392 | tf_op jit(solution)/shard_map/ppermute | solution.py:86
  109.2 1.0 add_convert_fusion.1
  110.3 2.7 %reshape.45 = bf16[16,16,1280]{2,1,0:T(8,128)(2,1)} reshape(bf16[80,4096]{1,0:T(8,128)(2,1)} %add_convert_fusion.1) | data formatting | bytes 1310720 | tf_op jit(solution)/shard_map/reshape | solution.py:88
  112.9 10.5 %all-to-all-start.1 = ((bf16[16,16,1280]{2,1,0:T(8,128)(2,1)}), bf16[16,16,1280]{2,1,0:T(8,128)(2,1)}, u32[]{:S(2)}, u32[]{:S(2)}) async-start(bf16[16,16,1280]{2,1,0:T(8,128)(2,1)} %reshape.45), calls=%async_computation.1 | async-start | bytes 1310720 | tf_op jit(solution)/shard_map/all_to_all | solution.py:89
  123.4 1.5 convolution_convert_fusion.1
  125.0 10.8 %collective-permute-start.5 = (bf16[192,1024]{1,0:T(8,128)(2,1)S(1)}, bf16[192,1024]{1,0:T(8,128)(2,1)S(1)}, u32[]{:S(2)}, u32[]{:S(2)}) collective-permute-start(bf16[192,1024]{1,0:T(8,128)(2,1)S(1)} %broadcast_select_fusion), channel_id=1, source_target_pairs={{0,448},{64,384},{128,320},{192,256},{256,192},{320,128},{384,64},... | collective-permute-start | bytes 1179656 | tf_op jit(solution)/shard_map/ppermute | solution.py:112
  135.8 56.2 %collective-permute-done.5 = bf16[192,1024]{1,0:T(8,128)(2,1)S(1)} collective-permute-done((bf16[192,1024]{1,0:T(8,128)(2,1)S(1)}, bf16[192,1024]{1,0:T(8,128)(2,1)S(1)}, u32[]{:S(2)}, u32[]{:S(2)}) %collective-permute-start.5) | collective-permute-done | bytes 393248 | tf_op jit(solution)/shard_map/ppermute | solution.py:112
  192.9 1.9 reshape.46
  194.8 1.1 convolution_convert_fusion.2
  195.9 1.4 convolution_convert_fusion.3
  (45 shorter events, 9.1 us)
Async XLA Ops:
  0.6 81.0 %copy-start = (bf16[1,2048,192]{1,2,0:T(8,128)(2,1)S(1)}, bf16[1,2048,192]{1,2,0:T(8,128)(2,1)}, u32[]{:S(2)}) copy-start(bf16[1,2048,192]{1,2,0:T(8,128)(2,1)} %param.12) | copy-start | bytes 2359300
  51.6 17.5 %collective-permute-start = (bf16[16,16,1280]{2,1,0:T(8,128)(2,1)S(1)}, bf16[16,16,1280]{2,1,0:T(8,128)(2,1)S(1)}, u32[]{:S(2)}, u32[]{:S(2)}) collective-permute-start(bf16[16,16,1280]{2,1,0:T(8,128)(2,1)S(1)} %all_to_all.10), channel_id=1, source_target_pairs={{0,2},{2,0},{1,3},{3,1},{4,6},{6,4},{5,7},{7,5},{8,10},{10,8},{9,1... | collective-permute-start | bytes 1966088 | tf_op jit(solution)/shard_map/ppermute | solution.py:72
  54.1 17.0 %collective-permute-start.1 = (bf16[16,16,1280]{2,1,0:T(8,128)(2,1)S(1)}, bf16[16,16,1280]{2,1,0:T(8,128)(2,1)S(1)}, u32[]{:S(2)}, u32[]{:S(2)}) collective-permute-start(bf16[16,16,1280]{2,1,0:T(8,128)(2,1)S(1)} %all_to_all.10), channel_id=1, source_target_pairs={{0,1},{1,0},{2,3},{3,2},{4,5},{5,4},{6,7},{7,6},{8,9},{9,8},{10,11... | collective-permute-start | bytes 1966088 | tf_op jit(solution)/shard_map/ppermute | solution.py:73
  69.1 4.0 %collective-permute-start.2 = (bf16[16,16,1280]{2,1,0:T(8,128)(2,1)S(1)}, bf16[16,16,1280]{2,1,0:T(8,128)(2,1)S(1)}, u32[]{:S(2)}, u32[]{:S(2)}) collective-permute-start(bf16[16,16,1280]{2,1,0:T(8,128)(2,1)S(1)} %collective-permute-done), channel_id=1, source_target_pairs={{0,1},{1,0},{2,3},{3,2},{4,5},{5,4},{6,7},{7,6},{8,9},{9,8},{10,11... | collective-permute-start | bytes 1966088 | tf_op jit(solution)/shard_map/ppermute | solution.py:74
  77.5 2.4 %copy-start.1 = (bf16[320,4096]{1,0:T(8,128)(2,1)S(1)}, bf16[320,4096]{1,0:T(8,128)(2,1)}, u32[]{:S(2)}) copy-start(bf16[320,4096]{1,0:T(8,128)(2,1)} %reshape.44) | copy-start | bytes 7864324
  81.7 1.1 copy-start.3
  82.4 1.6 copy-start.5
  83.4 1.1 copy-start.4
  85.2 4.9 %collective-permute-start.3 = (bf16[160,4096]{1,0:T(8,128)(2,1)S(1)}, bf16[160,4096]{1,0:T(8,128)(2,1)S(1)}, u32[]{:S(2)}, u32[]{:S(2)}) collective-permute-start(bf16[160,4096]{1,0:T(8,128)(2,1)S(1)} %pad_maximum_fusion.1), channel_id=1, source_target_pairs={{0,1},{1,0},{2,3},{3,2},{4,5},{5,4},{6,7},{7,6},{8,9},{9,8},{10,11... | collective-permute-start | bytes 3932168 | tf_op jit(solution)/shard_map/ppermute | solution.py:83
  90.6 18.7 %collective-permute-start.4 = (bf16[80,4096]{1,0:T(8,128)(2,1)S(1)}, bf16[80,4096]{1,0:T(8,128)(2,1)S(1)}, u32[]{:S(2)}, u32[]{:S(2)}) collective-permute-start(bf16[80,4096]{1,0:T(8,128)(2,1)S(1)} %slice.53), channel_id=1, source_target_pairs={{0,2},{2,0},{1,3},{3,1},{4,6},{6,4},{5,7},{7,5},{8,10},{10,8},{9,1... | collective-permute-start | bytes 1966088 | tf_op jit(solution)/shard_map/ppermute | solution.py:86
  112.9 80.0 %all-to-all-start.1 = ((bf16[16,16,1280]{2,1,0:T(8,128)(2,1)}), bf16[16,16,1280]{2,1,0:T(8,128)(2,1)}, u32[]{:S(2)}, u32[]{:S(2)}) async-start(bf16[16,16,1280]{2,1,0:T(8,128)(2,1)} %reshape.45), calls=%async_computation.1 | async-start | bytes 1310720 | tf_op jit(solution)/shard_map/all_to_all | solution.py:89
  124.9 72.4 %copy-start.2 = (f32[80,2048]{1,0:T(8,128)S(1)}, f32[80,2048]{1,0:T(8,128)}, u32[]{:S(2)}) copy-start(f32[80,2048]{1,0:T(8,128)} %get-tuple-element.5) | copy-start | bytes 1966084
  124.9 72.7 %copy-start.6 = (s32[128,8]{0,1:T(8,128)S(1)}, s32[128,8]{0,1:T(8,128)}, u32[]{:S(2)}) copy-start(s32[128,8]{0,1:T(8,128)} %param.9) | copy-start | bytes 12292
  125.0 67.0 %collective-permute-start.5 = (bf16[192,1024]{1,0:T(8,128)(2,1)S(1)}, bf16[192,1024]{1,0:T(8,128)(2,1)S(1)}, u32[]{:S(2)}, u32[]{:S(2)}) collective-permute-start(bf16[192,1024]{1,0:T(8,128)(2,1)S(1)} %broadcast_select_fusion), channel_id=1, source_target_pairs={{0,448},{64,384},{128,320},{192,256},{256,192},{320,128},{384,64},... | collective-permute-start | bytes 1179656 | tf_op jit(solution)/shard_map/ppermute | solution.py:112
